TPU v7x, 256 devices: a whole 4x4x8 slice. The times are simulated.
256 devices in a mesh: row: 8 (over x, core), col: 32 (over y, z).
Axes of the slice: x: 4, y: 4, z: 8, core: 2. Of those that a mesh axis runs over, the one named last changes fastest.
Arguments:
- features: bfloat16 [262144, 256], P(('row', 'col')), may hold values from -6 to 6
- weight: bfloat16 [256, 256], replicated, may hold values from -0.375 to 0.375
- layer_bias: float32 [256], replicated, may hold values from -3 to 3
- adj_tiles: bfloat16 [12288, 128, 128], P(('row', 'col')), may hold values from 0 to 0.079589844
- tile_source: int32 [12288], P(('row', 'col')), may hold values from 0 to 23, as said below
- tile_target: int32 [12288], P(('row', 'col')), may hold values from 0 to 95, as said below
- tile_count: int32 [256], P(('row', 'col')), may hold values from 1 to 48, as said below
- fetch_list: int32 [2048, 3], P(('row', 'col')), may hold values from -1 to 7, as said below
- deliver_list: int32 [8192, 3], P(('row', 'col')), may hold values from -1 to 7, as said below
- cotangent: bfloat16 [262144, 256], P(('row', 'col')), may hold values from -6 to 6
Outputs:
- layer_out: bfloat16 [262144, 256], P(('row', 'col'))
- grad_features: bfloat16 [262144, 256], P(('row', 'col'))
- grad_weight: float32 [256, 256], replicated
- grad_bias: float32 [256], replicated
Inputs may be any that keep to these rules, and one draw needn't show every extreme that they name: `tile_source`: each entry names a source slot q * 3 + j of its device whose fetch_list entry is not -1. `tile_target`: each entry names a row slot p * 3 + j of its device whose deliver_list entry is not -1. `tile_count`: live tiles are the first ones of a device; in every draw some device has 48 live tiles. `fetch_list`: each list holds one or more distinct local block numbers, then -1 in its unused slots; in every draw some device has all its lists full. `deliver_list`: each list holds one or more distinct local block numbers, then -1 in its unused slots; in every draw some owner has all its lists full.
All inputs are finite; a program needn't handle non-finite values.
Results may differ from a plain program's by a relative error of at most 0.0085.
Values may be sent and summed in bfloat16 or wider, within the bound.
No kernel may reach another device: no remote copies, remote signals or barrier semaphores. Data moves between devices by JAX's collectives and lax.ppermute only.
A program may use at most 128 MiB of HBM per device.

v0:
```python
import math

import jax
import jax.numpy as jnp
from jax import lax
from jax.sharding import PartitionSpec as P


def silu_grad(values):
    logistic = jax.nn.sigmoid(values)
    return logistic * (1.0 + values * (1.0 - logistic))


def tile_sums(adj_tiles, operand, take_slot, put_slot, live_count, slot_total, transpose):
    pattern = "kji,kjf->kif" if transpose else "kij,kjf->kif"
    tile_total = adj_tiles.shape[0]
    live_mask = jnp.arange(tile_total, dtype=jnp.int32) < live_count
    products = jnp.einsum(
        pattern, adj_tiles, operand[take_slot], preferred_element_type=jnp.float32
    )
    products = jnp.where(live_mask[:, None, None], products, 0.0)
    return jax.ops.segment_sum(products, put_slot, num_segments=slot_total)


def body(
    features,
    weight,
    layer_bias,
    adj_tiles,
    tile_source,
    tile_target,
    tile_count,
    fetch_list,
    deliver_list,
    cotangent,
):
    row_devices = lax.axis_size("row")
    col_devices = lax.axis_size("col")
    node_rows, feat_width = features.shape
    tile_side = adj_tiles.shape[1]
    own_blocks = node_rows // tile_side
    fetch_cap = fetch_list.shape[1]
    deliver_cap = deliver_list.shape[1]
    block_cells = tile_side * feat_width
    live_count = tile_count[0]
    projected = jnp.dot(features, weight, preferred_element_type=jnp.float32).astype(jnp.bfloat16)
    column = lax.all_gather(projected, "row", axis=0, tiled=True)
    source_operand = column.reshape(row_devices * own_blocks, tile_side, feat_width)
    global_ids = (
        jnp.arange(row_devices, dtype=jnp.int32)[:, None] * own_blocks + jnp.maximum(fetch_list, 0)
    ).reshape(-1)
    take_src = global_ids[tile_source]
    row_sums = tile_sums(
        adj_tiles,
        source_operand,
        take_src,
        tile_target,
        live_count,
        col_devices * deliver_cap,
        False,
    )
    outgoing_rows = row_sums.astype(jnp.bfloat16).reshape(col_devices, deliver_cap, block_cells)
    incoming = lax.all_to_all(outgoing_rows, "col", split_axis=0, concat_axis=0, tiled=True)
    deliver_hot = (
        deliver_list.reshape(-1)[None, :] == jnp.arange(own_blocks, dtype=jnp.int32)[:, None]
    ).astype(jnp.bfloat16)
    aggregated = jnp.dot(
        deliver_hot,
        incoming.reshape(col_devices * deliver_cap, block_cells),
        preferred_element_type=jnp.float32,
    )
    pre_act = aggregated.reshape(node_rows, feat_width) + layer_bias
    layer_out = jax.nn.silu(pre_act).astype(jnp.bfloat16)
    slopes = cotangent.astype(jnp.float32) * silu_grad(pre_act)
    bias_term = jnp.sum(slopes, axis=0)
    slope_blocks = slopes.astype(jnp.bfloat16).reshape(own_blocks, tile_side, feat_width)
    wanted_rows = slope_blocks[jnp.maximum(deliver_list, 0).reshape(-1)].reshape(
        col_devices, deliver_cap, tile_side, feat_width
    )
    row_values = lax.all_to_all(
        wanted_rows, "col", split_axis=0, concat_axis=0, tiled=True
    ).reshape(col_devices * deliver_cap, tile_side, feat_width)
    src_sums = tile_sums(
        adj_tiles, row_values, tile_target, tile_source, live_count, row_devices * fetch_cap, True
    )
    rounded = src_sums.astype(jnp.bfloat16).reshape(row_devices * fetch_cap, block_cells)
    valid_slots = fetch_list.reshape(-1) >= 0
    onehot = (
        (global_ids[None, :] == jnp.arange(row_devices * own_blocks, dtype=jnp.int32)[:, None])
        & valid_slots[None, :]
    ).astype(jnp.bfloat16)
    dense_rows = jnp.dot(onehot, rounded, preferred_element_type=jnp.float32)
    owned_sums = lax.psum_scatter(
        dense_rows.astype(jnp.bfloat16), "row", scatter_dimension=0, tiled=True
    ).astype(jnp.float32)
    grad_proj = owned_sums.reshape(node_rows, feat_width).astype(jnp.bfloat16)
    grad_features = jnp.dot(grad_proj, weight.T, preferred_element_type=jnp.float32).astype(
        jnp.bfloat16
    )
    weight_term = lax.dot_general(
        features, grad_proj, (((0,), (0,)), ((), ())), preferred_element_type=jnp.float32
    )
    grad_weight, grad_bias = lax.psum((weight_term, bias_term), ("row", "col"))
    grad_scale = 1.0 / math.sqrt(node_rows * row_devices * col_devices)
    return (layer_out, grad_features, grad_weight * grad_scale, grad_bias * grad_scale)


def solution(mesh):
    return jax.shard_map(
        body,
        mesh=mesh,
        in_specs=(
            P(("row", "col"), None),
            P(),
            P(),
            P(("row", "col"), None, None),
            P(("row", "col")),
            P(("row", "col")),
            P(("row", "col")),
            P(("row", "col"), None),
            P(("row", "col"), None),
            P(("row", "col"), None),
        ),
        out_specs=(P(("row", "col"), None), P(("row", "col"), None), P(), P()),
        check_vma=False,
    )
```

profile of v0, /device:TPU:1, one launch (start us, length us, event | category | flops | bytes accessed | tf_op | source)
XLA Modules:
  0.0 866.9 jit_solution(9749861221847638322)
XLA Ops:
  7.2 0.0 copy-start
  7.2 0.0 all-gather.2.cloned.1.call-start
  7.2 2.3 convolution_convert_fusion.2
  9.5 0.0 all-gather.2.cloned.1.call-update
  9.5 0.7 maximum_add_fusion
  10.2 0.1 copy.22
  10.3 0.1 reshape.102
  11.0 0.7 compare_select_fusion.3
  11.7 0.8 gather_fusion
  12.5 36.7 %all-gather.2.cloned.1.call-done = bf16[8192,256]{1,0:T(8,128)(2,1)} async-done(((bf16[1024,256]{1,0:T(8,128)(2,1)}), bf16[8192,256]{1,0:T(8,128)(2,1)}) %all-gather.2.cloned.1.call-update) | async-done | bytes 4194320 | tf_op jit(solution)/shard_map/all_gather | solution.py:47
  49.2 4.7 gather_fusion.1
  54.0 0.0 copy-done
  54.0 5.9 select_bitcast_fusion.1
  59.9 6.6 copy.24
  66.4 0.0 copy-start.6
  66.4 6.1 broadcast_in_dim.43
  72.5 0.0 copy-done.6
  72.5 14.8 %scatter_fusion = f32[96,128,256]{2,1,0:T(8,128)} fusion(f32[96,128,256]{2,1,0:T(8,128)} %broadcast_in_dim.43, s32[48]{0:T(128)S(1)} %copy-done.6, f32[48,128,256]{2,1,0:T(8,128)} %copy.24), kind=kCustom, calls=%fused_computation.4 | custom fusion | flops 1572864 | bytes 18874560 | tf_op jit(solution)/shard_map/scatter-add | solution.py:22
  87.3 8.2 convert_element_type.32
  95.5 12.3 %reshape.103 = bf16[32,3,32768]{2,1,0:T(4,128)(2,1)} reshape(bf16[96,128,256]{2,1,0:T(8,128)(2,1)} %convert_element_type.32) | data formatting | bytes 12582912 | tf_op jit(solution)/shard_map/reshape | solution.py:62
  107.8 0.0 copy-start.3
  107.8 9.9 %all-to-all-start = ((bf16[32,3,32768]{2,1,0:T(4,128)(2,1)}), bf16[32,3,32768]{2,1,0:T(4,128)(2,1)}, u32[]{:S(2)}, u32[]{:S(2)}) async-start(bf16[32,3,32768]{2,1,0:T(4,128)(2,1)} %reshape.103), calls=%async_computation | async-start | bytes 16777216 | tf_op jit(solution)/shard_map/all_to_all | solution.py:63
  117.7 0.0 copy-done.3
  117.7 0.1 copy.21
  117.8 0.1 eq.28
  117.9 0.1 copy.26
  118.0 0.1 reshape.107
  118.1 189.8 %all-to-all-done = bf16[32,3,32768]{2,1,0:T(4,128)(2,1)} async-done(((bf16[32,3,32768]{2,1,0:T(4,128)(2,1)}), bf16[32,3,32768]{2,1,0:T(4,128)(2,1)}, u32[]{:S(2)}, u32[]{:S(2)}) %all-to-all-start) | async-done | bytes 6291488 | tf_op jit(solution)/shard_map/all_to_all | solution.py:63
  307.9 9.0 %reshape.104 = bf16[96,32768]{1,0:T(8,128)(2,1)} reshape(bf16[32,3,32768]{2,1,0:T(4,128)(2,1)} %all-to-all-done) | data formatting | bytes 12582912 | tf_op jit(solution)/shard_map/reshape | solution.py:69
  316.9 0.0 copy-start.5
  316.9 4.7 fusion.4
  321.6 1.4 reshape.105
  323.0 0.0 copy-done.5
  323.0 2.4 fusion.8
  325.3 6.0 gather_fusion.2
  331.3 12.6 %all-to-all-start.1 = ((bf16[32,3,128,256]{3,2,1,0:T(8,128)(2,1)}), bf16[32,3,128,256]{3,2,1,0:T(8,128)(2,1)}, u32[]{:S(2)}, u32[]{:S(2)}) async-start(bf16[32,3,128,256]{3,2,1,0:T(8,128)(2,1)} %bitcast.33), calls=%async_computation.1 | async-start | bytes 12582912 | tf_op jit(solution)/shard_map/all_to_all | solution.py:80
  343.9 0.2 reduce-scatter.2.cloned.1.call-start
  344.1 0.0 copy-done.4
  344.1 0.1 copy.25
  344.2 0.1 ge.11
  344.3 138.6 %all-to-all-done.1 = bf16[32,3,128,256]{3,2,1,0:T(8,128)(2,1)} async-done(((bf16[32,3,128,256]{3,2,1,0:T(8,128)(2,1)}), bf16[32,3,128,256]{3,2,1,0:T(8,128)(2,1)}, u32[]{:S(2)}, u32[]{:S(2)}) %all-to-all-start.1) | async-done | bytes 6291488 | tf_op jit(solution)/shard_map/all_to_all | solution.py:80
  482.9 5.3 gather_fusion.3
  488.2 5.9 select_bitcast_fusion
  494.1 6.6 copy.28
  500.7 2.0 broadcast_in_dim.48
  502.8 0.0 copy-done.7
  502.8 14.2 %scatter_fusion.1 = f32[24,128,256]{2,1,0:T(8,128)} fusion(f32[24,128,256]{2,1,0:T(8,128)} %broadcast_in_dim.48, s32[48]{0:T(128)S(1)} %copy-done.7, f32[48,128,256]{2,1,0:T(8,128)} %copy.28), kind=kCustom, calls=%fused_computation.5 | custom fusion | flops 1572864 | bytes 18874560 | tf_op jit(solution)/shard_map/scatter-add | solution.py:22
  517.0 2.1 convert_element_type.36
  519.1 0.9 copy.32
  520.0 0.0 copy-start.1
  520.0 3.2 convolution_convert_fusion
  523.2 0.0 reduce-scatter.2.cloned.1.call-update
  523.2 0.0 all-reduce.2.cloned.1.call-start
  523.2 83.6 %psum.15 = f32[256]{0:T(256)S(1)} all-reduce(f32[256]{0:T(256)S(1)} %get-tuple-element.12), channel_id=1, replica_groups=mesh['row'=8,'col'=32] {'row','col'}, use_global_device_ids=true, to_apply=%region_5.6 | all-reduce | flops 256 | bytes 2048 | tf_op jit(solution)/shard_map/psum | solution.py:103
  606.8 0.6 broadcast_multiply_fusion.1
  607.4 1.3 convert_element_type.38
  608.7 0.0 copy-done.1
  608.7 1.0 convolution_bitcast_fusion
  609.7 0.0 all-reduce.2.cloned.1.call-update
  609.7 0.0 copy-done.2
  609.8 1.1 convolution_convert_fusion.1
  610.9 247.7 %all-reduce.2.cloned.1.call-done = f32[256,256]{0,1:T(8,128)} async-done(((f32[256,256]{0,1:T(8,128)}), f32[256,256]{0,1:T(8,128)}) %all-reduce.2.cloned.1.call-update) | async-done | bytes 262160 | tf_op jit(solution)/shard_map/psum | solution.py:103
  858.6 1.0 broadcast_multiply_fusion
  859.6 0.8 copy.29
  (15 shorter events, 0.1 us)
Async XLA Ops:
  7.2 46.8 %copy-start = (bf16[48,128,128]{2,1,0:T(8,128)(2,1)S(1)}, bf16[48,128,128]{2,1,0:T(8,128)(2,1)}, u32[]{:S(2)}) copy-start(bf16[48,128,128]{2,1,0:T(8,128)(2,1)} %param.13) | copy-start | bytes 4718596
  7.2 42.0 %all-gather.2.cloned.1.call-start = ((), (), s32[]{:S(2)}) async-start(), calls=%async_computation.3 | async-start | bytes 4718592 | tf_op jit(solution)/shard_map/all_gather | solution.py:47
  66.4 6.1 copy-start.6
  107.8 9.9 %copy-start.3 = (s32[32,3]{0,1:T(4,128)S(1)}, s32[32,3]{0,1:T(4,128)}, u32[]{:S(2)}) copy-start(s32[32,3]{0,1:T(4,128)} %param.18) | copy-start | bytes 1156
  107.8 200.1 %all-to-all-start = ((bf16[32,3,32768]{2,1,0:T(4,128)(2,1)}), bf16[32,3,32768]{2,1,0:T(4,128)(2,1)}, u32[]{:S(2)}, u32[]{:S(2)}) async-start(bf16[32,3,32768]{2,1,0:T(4,128)(2,1)} %reshape.103), calls=%async_computation | async-start | bytes 16777216 | tf_op jit(solution)/shard_map/all_to_all | solution.py:63
  316.9 6.1 copy-start.5
  331.3 12.8 %copy-start.4 = (s32[8,3]{0,1:T(4,128)S(1)}, s32[8,3]{0,1:T(4,128)}, u32[]{:S(2)}) copy-start(s32[8,3]{0,1:T(4,128)} %param.17) | copy-start | bytes 292
  331.3 151.7 %all-to-all-start.1 = ((bf16[32,3,128,256]{3,2,1,0:T(8,128)(2,1)}), bf16[32,3,128,256]{3,2,1,0:T(8,128)(2,1)}, u32[]{:S(2)}, u32[]{:S(2)}) async-start(bf16[32,3,128,256]{3,2,1,0:T(8,128)(2,1)} %bitcast.33), calls=%async_computation.1 | async-start | bytes 12582912 | tf_op jit(solution)/shard_map/all_to_all | solution.py:80
  343.9 263.5 %reduce-scatter.2.cloned.1.call-start = ((), (), s32[]{:S(2)}) async-start(), calls=%async_computation.4 | async-start | bytes 4718592 | tf_op jit(solution)/shard_map/reduce_scatter | solution.py:93
  494.1 8.6 copy-start.7
  520.0 88.7 %copy-start.1 = (bf16[1024,256]{1,0:T(8,128)(2,1)S(1)}, bf16[1024,256]{1,0:T(8,128)(2,1)}, u32[]{:S(2)}) copy-start(bf16[1024,256]{1,0:T(8,128)(2,1)} %param.10) | copy-start | bytes 1572868
  523.2 86.6 %copy-start.2 = (bf16[256,256]{1,0:T(8,128)(2,1)S(1)}, bf16[256,256]{1,0:T(8,128)(2,1)}, u32[]{:S(2)}) copy-start(bf16[256,256]{1,0:T(8,128)(2,1)} %param.11) | copy-start | bytes 393220
  523.2 335.4 %all-reduce.2.cloned.1.call-start = ((), (), s32[]{:S(2)}) async-start(), calls=%async_computation.5 | async-start | bytes 524288 | tf_op jit(solution)/shard_map/psum | solution.py:103
Sparse Core Ops, SparseCore 0:
  10.4 38.7 all-gather.1
  523.3 44.2 reduce-scatter.1
  609.9 248.6 all-reduce.1
where the time goes:
time: 869 us; the launch traced here: 867 us
  waiting for transfers between devices  613 us (71%)
  blocking collectives  83.6 us (10%)
  local copies, waits for them, and re-layouts  64.5 us (7%)
  other arithmetic  44.5 us (5%)
  matrix products  24.1 us (3%)
  starting transfers between devices  22.8 us (3%)
  between operations  14.6 us (2%)
    psum x1, waiting for transfers between devices, body(): grad_weight, grad_bias = lax.psum((weight_term, bias_term), ('row', 'col'))  248 us
    all_to_all x1, waiting for transfers between devices, body(): lax.all_to_all(outgoing_rows, 'col', split_axis=0, concat_axis=0, tiled=T...  190 us
    all_to_all x1, waiting for transfers between devices, body(): lax.all_to_all(wanted_rows, 'col', split_axis=0, concat_axis=0, tiled=True)  139 us
    psum x1, blocking collectives, body(): grad_weight, grad_bias = lax.psum((weight_term, bias_term), ('row', 'col'))  83.6 us
    all_gather x1, waiting for transfers between devices, body(): column = lax.all_gather(projected, 'row', axis=0, tiled=True)  36.7 us
    scatter-add x2, other arithmetic, tile_sums(): return jax.ops.segment_sum(products, put_slot, num_segments=slot_total)  29 us
  transfers between devices with their start and end apart: 5, of which 4 were waited for; matrix products, arithmetic and copies ran while one was open for 1% of the time, Pallas kernels for 0%

commit v1 on v0

--- a/solution.py
+++ b/solution.py
@@ -20,6 +20,22 @@
     )
     products = jnp.where(live_mask[:, None, None], products, 0.0)
     return jax.ops.segment_sum(products, put_slot, num_segments=slot_total)
+
+
+def all_sum(weight_term, bias_term):
+    devices = lax.axis_size(("row", "col"))
+    rows, width = weight_term.shape
+    packed = jnp.concatenate([weight_term, bias_term[None, :]], axis=0)
+    chunk = -(-(rows + 1) // devices)
+    packed = jnp.pad(packed, ((0, chunk * devices - rows - 1), (0, 0)))
+    parts = lax.all_to_all(
+        packed.reshape(devices, chunk, width), ("row", "col"), 0, 0, tiled=True
+    )
+    owned = jnp.sum(parts, axis=0)
+    spread = lax.all_to_all(
+        jnp.broadcast_to(owned[None], (devices, chunk, width)), ("row", "col"), 0, 0, tiled=True
+    ).reshape(devices * chunk, width)
+    return spread[:rows], spread[rows]
 
 
 def body(
@@ -100,7 +116,7 @@
     weight_term = lax.dot_general(
         features, grad_proj, (((0,), (0,)), ((), ())), preferred_element_type=jnp.float32
     )
-    grad_weight, grad_bias = lax.psum((weight_term, bias_term), ("row", "col"))
+    grad_weight, grad_bias = all_sum(weight_term, bias_term)
     grad_scale = 1.0 / math.sqrt(node_rows * row_devices * col_devices)
     return (layer_out, grad_features, grad_weight * grad_scale, grad_bias * grad_scale)
 

time: 869 us -> 642 us (0.74)
  waiting for transfers between devices: 613 us -> 421 us
  blocking collectives: 83.6 us -> 34.6 us
  starting transfers between devices: 22.8 us -> 36.8 us
    psum x1 -> x0, waiting for transfers between devices: 248 us -> none  [body(): grad_weight, grad_bias = lax.psum((weight_term, bias_term), ('row', 'col'))]
    psum x1 -> x0, blocking collectives: 83.6 us -> none  [body(): grad_weight, grad_bias = lax.psum((weight_term, bias_term), ('row', 'col'))]
    reduce_scatter x1, waiting for transfers between devices: 0.01 us -> 37.9 us  [body(): lax.psum_scatter(dense_rows.astype(jnp.bfloat16), 'row', scatter_dimensio...]
    all_to_all x0 -> x1, blocking collectives: none -> 34.6 us  [all_sum(): lax.all_to_all(packed.reshape(devices, chunk, width), ('row', 'col'), 0,...]
    all_to_all x0 -> x1, waiting for transfers between devices: none -> 20.3 us  [all_sum(): lax.all_to_all(jnp.broadcast_to(owned[None], (devices, chunk, width)), ('...]
  transfers between devices with their start and end apart: 5 -> 5, of which waited for: 4 -> 5; matrix products, arithmetic and copies ran while one was open for 1% -> 1% of each run, Pallas kernels for 0% -> 0%
where the time goes in v1:
time: 642 us; the launch traced here: 641 us
  waiting for transfers between devices  421 us (66%)
  local copies, waits for them, and re-layouts  66.2 us (10%)
  other arithmetic  44 us (7%)
  starting transfers between devices  36.8 us (6%)
  blocking collectives  34.6 us (5%)
  matrix products  23.4 us (4%)
  between operations  14.9 us (2%)
    all_to_all x1, waiting for transfers between devices, body(): lax.all_to_all(outgoing_rows, 'col', split_axis=0, concat_axis=0, tiled=T...  189 us
    all_to_all x1, waiting for transfers between devices, body(): lax.all_to_all(wanted_rows, 'col', split_axis=0, concat_axis=0, tiled=True)  138 us
    reduce_scatter x1, waiting for transfers between devices, body(): lax.psum_scatter(dense_rows.astype(jnp.bfloat16), 'row', scatter_dimensio...  37.9 us
    all_gather x1, waiting for transfers between devices, body(): column = lax.all_gather(projected, 'row', axis=0, tiled=True)  36.7 us
    all_to_all x1, blocking collectives, all_sum(): lax.all_to_all(packed.reshape(devices, chunk, width), ('row', 'col'), 0,...  34.6 us
    scatter-add x2, other arithmetic, tile_sums(): return jax.ops.segment_sum(products, put_slot, num_segments=slot_total)  29 us
    all_to_all x1, starting transfers between devices, body(): lax.all_to_all(wanted_rows, 'col', split_axis=0, concat_axis=0, tiled=True)  21.3 us
    all_to_all x1, waiting for transfers between devices, all_sum(): lax.all_to_all(jnp.broadcast_to(owned[None], (devices, chunk, width)), ('...  20.3 us
  transfers between devices with their start and end apart: 5, of which 5 were waited for; matrix products, arithmetic and copies ran while one was open for 1% of the time, Pallas kernels for 0%

profile of v1, /device:TPU:1, one launch (start us, length us, event | category | flops | bytes accessed | tf_op | source)
XLA Modules:
  0.0 641.3 jit_solution(13166882898423625455)
XLA Ops:
  7.2 0.0 copy-start
  7.2 0.0 all-gather.2.cloned.1.call-start
  7.2 2.3 convolution_convert_fusion.2
  9.5 0.0 all-gather.2.cloned.1.call-update
  9.5 0.7 maximum_add_fusion
  10.2 0.1 copy.21
  10.3 0.1 reshape.114
  11.0 0.7 compare_select_fusion.3
  11.7 0.8 gather_fusion
  12.5 36.7 %all-gather.2.cloned.1.call-done = bf16[8192,256]{1,0:T(8,128)(2,1)} async-done(((bf16[1024,256]{1,0:T(8,128)(2,1)}), bf16[8192,256]{1,0:T(8,128)(2,1)}) %all-gather.2.cloned.1.call-update) | async-done | bytes 4194320 | tf_op jit(solution)/shard_map/all_gather | solution.py:63
  49.2 4.7 gather_fusion.1
  54.0 0.0 copy-done
  54.0 5.9 select_bitcast_fusion.1
  59.9 6.6 %copy.23 = f32[48,128,256]{2,1,0:T(8,128)} copy(f32[48,128,256]{1,2,0:T(8,128)} %select_bitcast_fusion.1) | data formatting | bytes 12582912 | tf_op jit(solution)/shard_map/jit(_where)/select_n | solution.py:21
  66.5 6.1 broadcast_in_dim.52
  72.6 0.0 copy-done.6
  72.6 14.7 %scatter_fusion = f32[96,128,256]{2,1,0:T(8,128)} fusion(f32[96,128,256]{2,1,0:T(8,128)} %broadcast_in_dim.52, s32[48]{0:T(128)S(1)} %copy-done.6, f32[48,128,256]{2,1,0:T(8,128)} %copy.23), kind=kCustom, calls=%fused_computation.4 | custom fusion | flops 1572864 | bytes 18874560 | tf_op jit(solution)/shard_map/scatter-add | solution.py:22
  87.3 8.2 %convert_element_type.34 = bf16[96,128,256]{2,1,0:T(8,128)(2,1)} convert(f32[96,128,256]{2,1,0:T(8,128)} %scatter_fusion) | non-fusion elementwise | flops 3145728 | bytes 18874368 | tf_op jit(solution)/shard_map/convert_element_type | solution.py:78
  95.5 12.3 %reshape.115 = bf16[32,3,32768]{2,1,0:T(4,128)(2,1)} reshape(bf16[96,128,256]{2,1,0:T(8,128)(2,1)} %convert_element_type.34) | data formatting | bytes 12582912 | tf_op jit(solution)/shard_map/reshape | solution.py:78
  107.8 9.9 %all-to-all-start = ((bf16[32,3,32768]{2,1,0:T(4,128)(2,1)}), bf16[32,3,32768]{2,1,0:T(4,128)(2,1)}, u32[]{:S(2)}, u32[]{:S(2)}) async-start(bf16[32,3,32768]{2,1,0:T(4,128)(2,1)} %reshape.115), calls=%async_computation | async-start | bytes 16777216 | tf_op jit(solution)/shard_map/all_to_all | solution.py:79
  117.7 0.0 copy-done.3
  117.7 0.1 copy.20
  117.8 0.1 eq.28
  117.9 0.1 copy.25
  118.0 0.1 reshape.119
  118.1 188.6 %all-to-all-done = bf16[32,3,32768]{2,1,0:T(4,128)(2,1)} async-done(((bf16[32,3,32768]{2,1,0:T(4,128)(2,1)}), bf16[32,3,32768]{2,1,0:T(4,128)(2,1)}, u32[]{:S(2)}, u32[]{:S(2)}) %all-to-all-start) | async-done | bytes 6291488 | tf_op jit(solution)/shard_map/all_to_all | solution.py:79
  306.7 9.0 %reshape.116 = bf16[96,32768]{1,0:T(8,128)(2,1)} reshape(bf16[32,3,32768]{2,1,0:T(4,128)(2,1)} %all-to-all-done) | data formatting | bytes 12582912 | tf_op jit(solution)/shard_map/reshape | solution.py:85
  315.6 4.7 fusion.4
  320.3 1.4 reshape.117
  321.7 0.0 copy-done.5
  321.7 2.4 fusion.8
  324.1 5.9 gather_fusion.2
  330.0 21.3 %all-to-all-start.1 = ((bf16[32,3,128,256]{3,2,1,0:T(8,128)(2,1)}), bf16[32,3,128,256]{3,2,1,0:T(8,128)(2,1)}, u32[]{:S(2)}, u32[]{:S(2)}) async-start(bf16[32,3,128,256]{3,2,1,0:T(8,128)(2,1)} %bitcast.35), calls=%async_computation.1 | async-start | bytes 12582912 | tf_op jit(solution)/shard_map/all_to_all | solution.py:96
  351.3 0.2 reduce-scatter.2.cloned.1.call-start
  351.5 0.0 copy-done.4
  351.6 0.1 copy.24
  351.6 0.1 ge.11
  351.8 137.7 %all-to-all-done.1 = bf16[32,3,128,256]{3,2,1,0:T(8,128)(2,1)} async-done(((bf16[32,3,128,256]{3,2,1,0:T(8,128)(2,1)}), bf16[32,3,128,256]{3,2,1,0:T(8,128)(2,1)}, u32[]{:S(2)}, u32[]{:S(2)}) %all-to-all-start.1) | async-done | bytes 6291488 | tf_op jit(solution)/shard_map/all_to_all | solution.py:96
  489.5 5.3 gather_fusion.3
  494.8 5.9 select_bitcast_fusion
  500.7 6.6 %copy.27 = f32[48,128,256]{2,1,0:T(8,128)} copy(f32[48,128,256]{1,2,0:T(8,128)} %select_bitcast_fusion) | data formatting | bytes 12582912 | tf_op jit(solution)/shard_map/jit(_where)/select_n | solution.py:21
  507.3 2.1 broadcast_in_dim.57
  509.3 14.3 %scatter_fusion.1 = f32[24,128,256]{2,1,0:T(8,128)} fusion(f32[24,128,256]{2,1,0:T(8,128)} %broadcast_in_dim.57, s32[48]{0:T(128)S(1)} %copy-done.7, f32[48,128,256]{2,1,0:T(8,128)} %copy.27), kind=kCustom, calls=%fused_computation.5 | custom fusion | flops 1572864 | bytes 18874560 | tf_op jit(solution)/shard_map/scatter-add | solution.py:22
  523.6 2.1 convert_element_type.38
  525.7 0.9 copy.30
  526.6 0.0 copy-start.1
  526.6 3.2 convolution_convert_fusion
  529.8 0.0 reduce-scatter.2.cloned.1.call-update
  529.8 0.0 copy-start.2
  529.9 37.9 %reduce-scatter.2.cloned.1.call-done = bf16[8,32768]{1,0:T(8,128)(2,1)} async-done(((bf16[64,32768]{1,0:T(8,128)(2,1)}), bf16[8,32768]{1,0:T(8,128)(2,1)}) %reduce-scatter.2.cloned.1.call-update) | async-done | bytes 524304 | tf_op jit(solution)/shard_map/reduce_scatter | solution.py:109
  567.7 1.3 convert_element_type.40
  569.0 0.0 copy-done.1
  569.0 0.3 convolution_bitcast_fusion
  569.4 0.3 reshape.123
  569.8 34.6 %all_to_all.20 = f32[256,2,256]{2,1,0:T(2,128)S(1)} all-to-all(f32[256,2,256]{2,1,0:T(2,128)S(1)} %reshape.123), channel_id=1, replica_groups=mesh['row'=8,'col'=32] {'row','col'}, dimensions={0} | all-to-all | bytes 1048576 | tf_op jit(solution)/shard_map/all_to_all | solution.py:31
  604.4 0.3 reduce_sum.19
  604.7 0.9 broadcast_in_dim.61
  605.6 5.4 all-to-all-start.3
  611.1 1.1 convolution_convert_fusion.1
  612.2 20.3 %all-to-all-done.3 = f32[256,2,256]{2,1,0:T(2,128)S(1)} async-done(((f32[256,2,256]{2,1,0:T(2,128)}), f32[256,2,256]{2,1,0:T(2,128)S(1)}, u32[]{:S(2)}, u32[]{:S(2)}) %all-to-all-start.3) | async-done | bytes 524320 | tf_op jit(solution)/shard_map/all_to_all | solution.py:35
  632.5 0.4 reshape.124
  632.9 0.6 slice_multiply_fusion.1
  633.5 0.1 slice_multiply_fusion
  633.6 0.9 mul.46
  (19 shorter events, 0.1 us)
Async XLA Ops:
  7.2 46.8 %copy-start = (bf16[48,128,128]{2,1,0:T(8,128)(2,1)S(1)}, bf16[48,128,128]{2,1,0:T(8,128)(2,1)}, u32[]{:S(2)}) copy-start(bf16[48,128,128]{2,1,0:T(8,128)(2,1)} %param.13) | copy-start | bytes 4718596
  7.2 42.0 %all-gather.2.cloned.1.call-start = ((), (), s32[]{:S(2)}) async-start(), calls=%async_computation.5 | async-start | bytes 4718592 | tf_op jit(solution)/shard_map/all_gather | solution.py:63
  66.5 6.1 copy-start.6
  107.8 9.9 %copy-start.3 = (s32[32,3]{0,1:T(4,128)S(1)}, s32[32,3]{0,1:T(4,128)}, u32[]{:S(2)}) copy-start(s32[32,3]{0,1:T(4,128)} %param.18) | copy-start | bytes 1156
  107.8 198.9 %all-to-all-start = ((bf16[32,3,32768]{2,1,0:T(4,128)(2,1)}), bf16[32,3,32768]{2,1,0:T(4,128)(2,1)}, u32[]{:S(2)}, u32[]{:S(2)}) async-start(bf16[32,3,32768]{2,1,0:T(4,128)(2,1)} %reshape.115), calls=%async_computation | async-start | bytes 16777216 | tf_op jit(solution)/shard_map/all_to_all | solution.py:79
  315.6 6.1 copy-start.5
  330.0 21.5 %copy-start.4 = (s32[8,3]{0,1:T(4,128)S(1)}, s32[8,3]{0,1:T(4,128)}, u32[]{:S(2)}) copy-start(s32[8,3]{0,1:T(4,128)} %param.17) | copy-start | bytes 292
  330.0 159.5 %all-to-all-start.1 = ((bf16[32,3,128,256]{3,2,1,0:T(8,128)(2,1)}), bf16[32,3,128,256]{3,2,1,0:T(8,128)(2,1)}, u32[]{:S(2)}, u32[]{:S(2)}) async-start(bf16[32,3,128,256]{3,2,1,0:T(8,128)(2,1)} %bitcast.35), calls=%async_computation.1 | async-start | bytes 12582912 | tf_op jit(solution)/shard_map/all_to_all | solution.py:96
  351.3 216.4 %reduce-scatter.2.cloned.1.call-start = ((), (), s32[]{:S(2)}) async-start(), calls=%async_computation.6 | async-start | bytes 4718592 | tf_op jit(solution)/shard_map/reduce_scatter | solution.py:109
  500.7 8.7 %copy-start.7 = (s32[48]{0:T(128)S(1)}, s32[48]{0:T(128)}, u32[]{:S(2)}) copy-start(s32[48]{0:T(128)} %param.14) | copy-start | bytes 580
  526.6 42.4 %copy-start.1 = (bf16[1024,256]{1,0:T(8,128)(2,1)S(1)}, bf16[1024,256]{1,0:T(8,128)(2,1)}, u32[]{:S(2)}) copy-start(bf16[1024,256]{1,0:T(8,128)(2,1)} %param.10) | copy-start | bytes 1572868
  529.8 81.2 %copy-start.2 = (bf16[256,256]{1,0:T(8,128)(2,1)S(1)}, bf16[256,256]{1,0:T(8,128)(2,1)}, u32[]{:S(2)}) copy-start(bf16[256,256]{1,0:T(8,128)(2,1)} %param.11) | copy-start | bytes 393220
  605.6 26.9 %all-to-all-start.3 = ((f32[256,2,256]{2,1,0:T(2,128)}), f32[256,2,256]{2,1,0:T(2,128)S(1)}, u32[]{:S(2)}, u32[]{:S(2)}) async-start(f32[256,2,256]{2,1,0:T(2,128)} %broadcast_in_dim.61), calls=%async_computation.4 | async-start | bytes 1048576 | tf_op jit(solution)/shard_map/all_to_all | solution.py:35
Sparse Core Ops, SparseCore 0:
  10.4 38.7 all-gather.1
  530.0 37.7 reduce-scatter.1

commit v2 on v1

--- a/solution.py
+++ b/solution.py
@@ -75,7 +75,9 @@
         col_devices * deliver_cap,
         False,
     )
-    outgoing_rows = row_sums.astype(jnp.bfloat16).reshape(col_devices, deliver_cap, block_cells)
+    outgoing_rows = row_sums.astype(jnp.bfloat16).reshape(
+        col_devices, deliver_cap, tile_side, feat_width
+    )
     incoming = lax.all_to_all(outgoing_rows, "col", split_axis=0, concat_axis=0, tiled=True)
     deliver_hot = (
         deliver_list.reshape(-1)[None, :] == jnp.arange(own_blocks, dtype=jnp.int32)[:, None]

time: 642 us -> 566 us (0.88)
  waiting for transfers between devices: 421 us -> 375 us
  local copies, waits for them, and re-layouts: 66.2 us -> 51.8 us
  starting transfers between devices: 36.8 us -> 23.9 us
    all_to_all x1, waiting for transfers between devices: 189 us -> 140 us  [body(): lax.all_to_all(outgoing_rows, 'col', split_axis=0, concat_axis=0, tiled=T...]
    reshape x2 -> x0, local copies, waits for them, and re-layouts: 21.3 us -> none  [the longest x1 12.3 us: body(): row_sums.astype(jnp.bfloat16).reshape(col_devices, deliver_cap, block_cells)]
    all_to_all x1, starting transfers between devices: 21.3 us -> 8.39 us  [body(): lax.all_to_all(wanted_rows, 'col', split_axis=0, concat_axis=0, tiled=True)]
    unnamed x18 -> x19, local copies, waits for them, and re-layouts: 1.02 us -> 7.94 us
where the time goes in v2:
time: 566 us; the launch traced here: 565 us
  waiting for transfers between devices  375 us (66%)
  local copies, waits for them, and re-layouts  51.8 us (9%)
  other arithmetic  44.2 us (8%)
  blocking collectives  34.6 us (6%)
  starting transfers between devices  23.9 us (4%)
  matrix products  20.6 us (4%)
  between operations  14.9 us (3%)
    all_to_all x1, waiting for transfers between devices, body(): lax.all_to_all(outgoing_rows, 'col', split_axis=0, concat_axis=0, tiled=T...  140 us
    all_to_all x1, waiting for transfers between devices, body(): lax.all_to_all(wanted_rows, 'col', split_axis=0, concat_axis=0, tiled=True)  139 us
    reduce_scatter x1, waiting for transfers between devices, body(): lax.psum_scatter(dense_rows.astype(jnp.bfloat16), 'row', scatter_dimensio...  38.9 us
    all_gather x1, waiting for transfers between devices, body(): column = lax.all_gather(projected, 'row', axis=0, tiled=True)  36.7 us
    all_to_all x1, blocking collectives, all_sum(): lax.all_to_all(packed.reshape(devices, chunk, width), ('row', 'col'), 0,...  34.6 us
    scatter-add x2, other arithmetic, tile_sums(): return jax.ops.segment_sum(products, put_slot, num_segments=slot_total)  29.2 us
    all_to_all x1, waiting for transfers between devices, all_sum(): lax.all_to_all(jnp.broadcast_to(owned[None], (devices, chunk, width)), ('...  20.3 us
    select_n x2, local copies, waits for them, and re-layouts, tile_sums(): products = jnp.where(live_mask[:, None, None], products, 0.0)  13.2 us
  transfers between devices with their start and end apart: 5, of which 5 were waited for; matrix products, arithmetic and copies ran while one was open for 1% of the time, Pallas kernels for 0%

profile of v2, /device:TPU:1, one launch (start us, length us, event | category | flops | bytes accessed | tf_op | source)
XLA Modules:
  0.0 564.6 jit_solution(14171621038611908842)
XLA Ops:
  7.2 0.0 copy-start
  7.2 0.0 all-gather.2.cloned.1.call-start
  7.2 2.3 convolution_convert_fusion.2
  9.5 0.0 all-gather.2.cloned.1.call-update
  9.5 0.7 maximum_add_fusion
  10.2 0.1 copy.21
  10.3 0.1 reshape.114
  11.0 0.7 compare_select_fusion.3
  11.7 0.8 gather_fusion
  12.5 36.7 %all-gather.2.cloned.1.call-done = bf16[8192,256]{1,0:T(8,128)(2,1)} async-done(((bf16[1024,256]{1,0:T(8,128)(2,1)}), bf16[8192,256]{1,0:T(8,128)(2,1)}) %all-gather.2.cloned.1.call-update) | async-done | bytes 4194320 | tf_op jit(solution)/shard_map/all_gather | solution.py:63
  49.2 4.7 gather_fusion.1
  54.0 0.0 copy-done
  54.0 5.9 %select_bitcast_fusion.1 = f32[48,128,256]{1,2,0:T(8,128)} fusion(pred[48]{0:T(512)(128)(4,1)S(1)} %iota_compare_fusion.4, bf16[48,128,256]{2,1,0:T(8,128)(2,1)} %gather_fusion.1, bf16[48,128,128]{2,1,0:T(8,128)(2,1)S(1)} %copy-done), kind=kOutput, calls=%fused_computation.8 | convolution fusion | flops 404226048 | bytes 11010096 | tf_op jit(solution)/shard_map/kij,kjf->kif/dot_general | solution.py:18
  59.9 6.6 %copy.23 = f32[48,128,256]{2,1,0:T(8,128)} copy(f32[48,128,256]{1,2,0:T(8,128)} %select_bitcast_fusion.1) | data formatting | bytes 12582912 | tf_op jit(solution)/shard_map/jit(_where)/select_n | solution.py:21
  66.5 6.1 %broadcast_in_dim.52 = f32[96,128,256]{2,1,0:T(8,128)} broadcast(f32[]{:T(128)} %constant.8.clone.1), dimensions={} | broadcast | bytes 12582916 | tf_op jit(solution)/shard_map/broadcast_in_dim | solution.py:22
  72.6 0.0 copy-done.6
  72.6 14.9 %scatter_fusion = f32[96,128,256]{2,1,0:T(8,128)} fusion(f32[96,128,256]{2,1,0:T(8,128)} %broadcast_in_dim.52, s32[48]{0:T(128)S(1)} %copy-done.6, f32[48,128,256]{2,1,0:T(8,128)} %copy.23), kind=kCustom, calls=%fused_computation.4 | custom fusion | flops 1572864 | bytes 18874560 | tf_op jit(solution)/shard_map/scatter-add | solution.py:22
  87.4 8.1 %convert_element_type.34 = bf16[96,128,256]{2,1,0:T(8,128)(2,1)} convert(f32[96,128,256]{2,1,0:T(8,128)} %scatter_fusion) | non-fusion elementwise | flops 3145728 | bytes 18874368 | tf_op jit(solution)/shard_map/convert_element_type | solution.py:78
  95.6 9.8 %all-to-all-start = ((bf16[32,3,128,256]{3,2,1,0:T(8,128)(2,1)}), bf16[32,3,128,256]{3,2,1,0:T(8,128)(2,1)}, u32[]{:S(2)}, u32[]{:S(2)}) async-start(bf16[32,3,128,256]{3,2,1,0:T(8,128)(2,1)} %bitcast.40), calls=%async_computation | async-start | bytes 12582912 | tf_op jit(solution)/shard_map/all_to_all | solution.py:81
  105.4 0.0 copy-done.3
  105.4 0.1 copy.20
  105.5 0.1 eq.28
  105.6 0.1 copy.25
  105.7 0.1 reshape.119
  105.8 139.9 %all-to-all-done = bf16[32,3,128,256]{3,2,1,0:T(8,128)(2,1)} async-done(((bf16[32,3,128,256]{3,2,1,0:T(8,128)(2,1)}), bf16[32,3,128,256]{3,2,1,0:T(8,128)(2,1)}, u32[]{:S(2)}, u32[]{:S(2)}) %all-to-all-start) | async-done | bytes 6291488 | tf_op jit(solution)/shard_map/all_to_all | solution.py:81
  245.7 6.9 %copy.30 = bf16[12,8,128,256]{3,1,2,0:T(8,128)(2,1)S(1)} copy(bf16[12,8,128,256]{3,2,1,0:T(8,128)(2,1)} %bitcast.15) | data formatting | bytes 12582912
  252.7 0.0 copy-start.5
  252.7 1.9 fusion.4
  254.6 1.4 reshape.117
  256.0 0.0 copy-done.5
  256.0 2.4 fusion.8
  258.3 5.9 %gather_fusion.2 = bf16[96,128,256]{2,1,0:T(8,128)(2,1)} fusion(bf16[8,128,256]{2,1,0:T(8,128)(2,1)S(1)} %bitcast.38, s32[1024]{0:T(1024)S(1)} %pad_clamp_fusion.1), kind=kCustom, calls=%fused_computation.2 | custom fusion | bytes 12583296 | tf_op jit(solution)/shard_map/gather | solution.py:95
  264.3 8.4 %all-to-all-start.1 = ((bf16[32,3,128,256]{3,2,1,0:T(8,128)(2,1)}), bf16[32,3,128,256]{3,2,1,0:T(8,128)(2,1)}, u32[]{:S(2)}, u32[]{:S(2)}) async-start(bf16[32,3,128,256]{3,2,1,0:T(8,128)(2,1)} %bitcast.39), calls=%async_computation.1 | async-start | bytes 12582912 | tf_op jit(solution)/shard_map/all_to_all | solution.py:98
  272.7 0.3 reduce-scatter.2.cloned.1.call-start
  272.9 0.0 copy-done.4
  272.9 0.1 copy.24
  273.0 0.1 ge.11
  273.1 138.7 %all-to-all-done.1 = bf16[32,3,128,256]{3,2,1,0:T(8,128)(2,1)} async-done(((bf16[32,3,128,256]{3,2,1,0:T(8,128)(2,1)}), bf16[32,3,128,256]{3,2,1,0:T(8,128)(2,1)}, u32[]{:S(2)}, u32[]{:S(2)}) %all-to-all-start.1) | async-done | bytes 6291488 | tf_op jit(solution)/shard_map/all_to_all | solution.py:98
  411.8 5.3 gather_fusion.3
  417.1 5.9 %select_bitcast_fusion = f32[48,128,256]{1,2,0:T(8,128)} fusion(pred[48]{0:T(512)(128)(4,1)S(1)} %iota_compare_fusion.4, bf16[48,128,256]{2,1,0:T(8,128)(2,1)} %gather_fusion.3, bf16[48,128,128]{2,1,0:T(8,128)(2,1)S(1)} %copy-done), kind=kOutput, calls=%fused_computation.7 | convolution fusion | flops 404226048 | bytes 11010096 | tf_op jit(solution)/shard_map/kji,kjf->kif/dot_general | solution.py:18
  423.0 6.6 %copy.27 = f32[48,128,256]{2,1,0:T(8,128)} copy(f32[48,128,256]{1,2,0:T(8,128)} %select_bitcast_fusion) | data formatting | bytes 12582912 | tf_op jit(solution)/shard_map/jit(_where)/select_n | solution.py:21
  429.6 2.1 broadcast_in_dim.57
  431.7 14.3 %scatter_fusion.1 = f32[24,128,256]{2,1,0:T(8,128)} fusion(f32[24,128,256]{2,1,0:T(8,128)} %broadcast_in_dim.57, s32[48]{0:T(128)S(1)} %copy-done.7, f32[48,128,256]{2,1,0:T(8,128)} %copy.27), kind=kCustom, calls=%fused_computation.5 | custom fusion | flops 1572864 | bytes 18874560 | tf_op jit(solution)/shard_map/scatter-add | solution.py:22
  446.0 2.1 convert_element_type.38
  448.1 0.9 copy.31
  449.0 0.0 copy-start.1
  449.0 3.2 convolution_convert_fusion
  452.2 0.0 reduce-scatter.2.cloned.1.call-update
  452.2 0.0 copy-start.2
  452.2 38.9 %reduce-scatter.2.cloned.1.call-done = bf16[8,32768]{1,0:T(8,128)(2,1)} async-done(((bf16[64,32768]{1,0:T(8,128)(2,1)}), bf16[8,32768]{1,0:T(8,128)(2,1)}) %reduce-scatter.2.cloned.1.call-update) | async-done | bytes 524304 | tf_op jit(solution)/shard_map/reduce_scatter | solution.py:111
  491.1 1.3 convert_element_type.40
  492.4 0.3 convolution_bitcast_fusion
  492.8 0.3 reshape.123
  493.2 34.6 %all_to_all.20 = f32[256,2,256]{2,1,0:T(2,128)S(1)} all-to-all(f32[256,2,256]{2,1,0:T(2,128)S(1)} %reshape.123), channel_id=1, replica_groups=mesh['row'=8,'col'=32] {'row','col'}, dimensions={0} | all-to-all | bytes 1048576 | tf_op jit(solution)/shard_map/all_to_all | solution.py:31
  527.7 0.3 reduce_sum.19
  528.0 0.9 broadcast_in_dim.61
  528.9 5.4 all-to-all-start.3
  534.4 0.0 copy-done.2
  534.4 1.1 convolution_convert_fusion.1
  535.5 20.3 %all-to-all-done.3 = f32[256,2,256]{2,1,0:T(2,128)S(1)} async-done(((f32[256,2,256]{2,1,0:T(2,128)}), f32[256,2,256]{2,1,0:T(2,128)S(1)}, u32[]{:S(2)}, u32[]{:S(2)}) %all-to-all-start.3) | async-done | bytes 524320 | tf_op jit(solution)/shard_map/all_to_all | solution.py:35
  555.8 0.4 reshape.124
  556.2 0.6 slice_multiply_fusion.1
  556.8 0.1 slice_multiply_fusion
  556.9 0.9 mul.46
  (18 shorter events, 0.1 us)
Async XLA Ops:
  7.2 46.8 %copy-start = (bf16[48,128,128]{2,1,0:T(8,128)(2,1)S(1)}, bf16[48,128,128]{2,1,0:T(8,128)(2,1)}, u32[]{:S(2)}) copy-start(bf16[48,128,128]{2,1,0:T(8,128)(2,1)} %param.13) | copy-start | bytes 4718596
  7.2 42.0 %all-gather.2.cloned.1.call-start = ((), (), s32[]{:S(2)}) async-start(), calls=%async_computation.5 | async-start | bytes 4718592 | tf_op jit(solution)/shard_map/all_gather | solution.py:63
  66.5 6.1 %copy-start.6 = (s32[48]{0:T(128)S(1)}, s32[48]{0:T(128)}, u32[]{:S(2)}) copy-start(s32[48]{0:T(128)} %param.15) | copy-start | bytes 580
  95.6 9.8 %copy-start.3 = (s32[32,3]{0,1:T(4,128)S(1)}, s32[32,3]{0,1:T(4,128)}, u32[]{:S(2)}) copy-start(s32[32,3]{0,1:T(4,128)} %param.18) | copy-start | bytes 1156
  95.6 150.2 %all-to-all-start = ((bf16[32,3,128,256]{3,2,1,0:T(8,128)(2,1)}), bf16[32,3,128,256]{3,2,1,0:T(8,128)(2,1)}, u32[]{:S(2)}, u32[]{:S(2)}) async-start(bf16[32,3,128,256]{3,2,1,0:T(8,128)(2,1)} %bitcast.40), calls=%async_computation | async-start | bytes 12582912 | tf_op jit(solution)/shard_map/all_to_all | solution.py:81
  252.7 3.3 copy-start.5
  264.3 8.7 %copy-start.4 = (s32[8,3]{0,1:T(4,128)S(1)}, s32[8,3]{0,1:T(4,128)}, u32[]{:S(2)}) copy-start(s32[8,3]{0,1:T(4,128)} %param.17) | copy-start | bytes 292
  264.3 147.6 %all-to-all-start.1 = ((bf16[32,3,128,256]{3,2,1,0:T(8,128)(2,1)}), bf16[32,3,128,256]{3,2,1,0:T(8,128)(2,1)}, u32[]{:S(2)}, u32[]{:S(2)}) async-start(bf16[32,3,128,256]{3,2,1,0:T(8,128)(2,1)} %bitcast.39), calls=%async_computation.1 | async-start | bytes 12582912 | tf_op jit(solution)/shard_map/all_to_all | solution.py:98
  272.7 218.5 %reduce-scatter.2.cloned.1.call-start = ((), (), s32[]{:S(2)}) async-start(), calls=%async_computation.6 | async-start | bytes 4718592 | tf_op jit(solution)/shard_map/reduce_scatter | solution.py:111
  423.0 8.7 %copy-start.7 = (s32[48]{0:T(128)S(1)}, s32[48]{0:T(128)}, u32[]{:S(2)}) copy-start(s32[48]{0:T(128)} %param.14) | copy-start | bytes 580
  449.0 43.5 %copy-start.1 = (bf16[1024,256]{1,0:T(8,128)(2,1)S(1)}, bf16[1024,256]{1,0:T(8,128)(2,1)}, u32[]{:S(2)}) copy-start(bf16[1024,256]{1,0:T(8,128)(2,1)} %param.10) | copy-start | bytes 1572868
  452.2 82.2 %copy-start.2 = (bf16[256,256]{1,0:T(8,128)(2,1)S(1)}, bf16[256,256]{1,0:T(8,128)(2,1)}, u32[]{:S(2)}) copy-start(bf16[256,256]{1,0:T(8,128)(2,1)} %param.11) | copy-start | bytes 393220
  528.9 26.9 %all-to-all-start.3 = ((f32[256,2,256]{2,1,0:T(2,128)}), f32[256,2,256]{2,1,0:T(2,128)S(1)}, u32[]{:S(2)}, u32[]{:S(2)}) async-start(f32[256,2,256]{2,1,0:T(2,128)} %broadcast_in_dim.61), calls=%async_computation.4 | async-start | bytes 1048576 | tf_op jit(solution)/shard_map/all_to_all | solution.py:35
Sparse Core Ops, SparseCore 0:
  10.4 38.7 all-gather.1
  452.3 38.7 reduce-scatter.1

commit v3 on v2

--- a/solution.py
+++ b/solution.py
@@ -1,8 +1,11 @@
+import functools
 import math
 
 import jax
 import jax.numpy as jnp
 from jax import lax
+from jax.experimental import pallas as pl
+from jax.experimental.pallas import tpu as pltpu
 from jax.sharding import PartitionSpec as P
 
 
@@ -11,15 +14,48 @@
     return logistic * (1.0 + values * (1.0 - logistic))
 
 
+def tile_kernel(take_ref, put_ref, count_ref, adj_ref, operand_ref, out_ref, acc_ref, *, transpose):
+    acc_ref[...] = jnp.zeros_like(acc_ref)
+
+    def step(k, carry):
+        tile = adj_ref[k]
+        picked = operand_ref[take_ref[k]]
+        if transpose:
+            product = lax.dot_general(
+                tile, picked, (((0,), (0,)), ((), ())), preferred_element_type=jnp.float32
+            )
+        else:
+            product = jnp.dot(tile, picked, preferred_element_type=jnp.float32)
+        slot = put_ref[k]
+        acc_ref[slot] = acc_ref[slot] + product
+        return carry
+
+    lax.fori_loop(0, count_ref[0], step, 0)
+    out_ref[...] = acc_ref[...].astype(out_ref.dtype)
+
+
 def tile_sums(adj_tiles, operand, take_slot, put_slot, live_count, slot_total, transpose):
-    pattern = "kji,kjf->kif" if transpose else "kij,kjf->kif"
-    tile_total = adj_tiles.shape[0]
-    live_mask = jnp.arange(tile_total, dtype=jnp.int32) < live_count
-    products = jnp.einsum(
-        pattern, adj_tiles, operand[take_slot], preferred_element_type=jnp.float32
+    tile_side = adj_tiles.shape[1]
+    width = operand.shape[-1]
+    smem = pl.BlockSpec(memory_space=pltpu.SMEM)
+    vmem = pl.BlockSpec(memory_space=pltpu.VMEM)
+    flops = 2 * adj_tiles.shape[0] * tile_side * tile_side * width
+    moved = (adj_tiles.size + operand.size + slot_total * tile_side * width) * 2
+    return pl.pallas_call(
+        functools.partial(tile_kernel, transpose=transpose),
+        out_shape=jax.ShapeDtypeStruct((slot_total, tile_side, width), jnp.bfloat16),
+        in_specs=[smem, smem, smem, vmem, vmem],
+        out_specs=vmem,
+        scratch_shapes=[pltpu.VMEM((slot_total, tile_side, width), jnp.float32)],
+        compiler_params=pltpu.CompilerParams(vmem_limit_bytes=56 * 1024 * 1024),
+        cost_estimate=pl.CostEstimate(flops=flops, bytes_accessed=moved, transcendentals=0),
+    )(
+        take_slot.astype(jnp.int32),
+        put_slot.astype(jnp.int32),
+        jnp.reshape(live_count, (1,)).astype(jnp.int32),
+        adj_tiles,
+        operand,
     )
-    products = jnp.where(live_mask[:, None, None], products, 0.0)
-    return jax.ops.segment_sum(products, put_slot, num_segments=slot_total)
 
 
 def all_sum(weight_term, bias_term):
@@ -75,7 +111,7 @@
         col_devices * deliver_cap,
         False,
     )
-    outgoing_rows = row_sums.astype(jnp.bfloat16).reshape(
+    outgoing_rows = row_sums.reshape(
         col_devices, deliver_cap, tile_side, feat_width
     )
     incoming = lax.all_to_all(outgoing_rows, "col", split_axis=0, concat_axis=0, tiled=True)
@@ -101,7 +137,7 @@
     src_sums = tile_sums(
         adj_tiles, row_values, tile_target, tile_source, live_count, row_devices * fetch_cap, True
     )
-    rounded = src_sums.astype(jnp.bfloat16).reshape(row_devices * fetch_cap, block_cells)
+    rounded = src_sums.reshape(row_devices * fetch_cap, block_cells)
     valid_slots = fetch_list.reshape(-1) >= 0
     onehot = (
         (global_ids[None, :] == jnp.arange(row_devices * own_blocks, dtype=jnp.int32)[:, None])

time: 566 us -> 514 us (0.908)
  other arithmetic: 44.2 us -> 4.73 us
  local copies, waits for them, and re-layouts: 51.8 us -> 22.1 us
  Pallas kernels: 0 us -> 15.6 us
  matrix products: 20.6 us -> 7.58 us
  starting transfers between devices: 23.9 us -> 30.8 us
    scatter-add x2 -> x0, other arithmetic: 29.2 us -> none  [tile_sums(): return jax.ops.segment_sum(products, put_slot, num_segments=slot_total)]
    pallas_call x0 -> x2, Pallas kernels: none -> 15.6 us  [tile_sums(): pl.pallas_call(functools.partial(tile_kernel, transpose=transpose), out_s...]
    select_n x2 -> x0, local copies, waits for them, and re-layouts: 13.2 us -> none  [tile_sums(): products = jnp.where(live_mask[:, None, None], products, 0.0)]
    dot_general x2 -> x0, matrix products: 11.8 us -> none  [tile_sums(): jnp.einsum(pattern, adj_tiles, operand[take_slot], preferred_element_type...]
    convert_element_type x2 -> x0, other arithmetic: 10.2 us -> none  [the longest x1 8.13 us: body(): row_sums.astype(jnp.bfloat16)]
    gather x2 -> x0, local copies, waits for them, and re-layouts: 10 us -> none  [tile_sums(): operand[take_slot]]
    broadcast_in_dim x2 -> x0, local copies, waits for them, and re-layouts: 8.16 us -> none  [tile_sums(): return jax.ops.segment_sum(products, put_slot, num_segments=slot_total)]
where the time goes in v3:
time: 514 us; the launch traced here: 510 us
  waiting for transfers between devices  380 us (74%)
  blocking collectives  34.6 us (7%)
  starting transfers between devices  30.8 us (6%)
  local copies, waits for them, and re-layouts  22.1 us (4%)
  Pallas kernels  15.6 us (3%)
  between operations  14.9 us (3%)
  matrix products  7.58 us (1%)
    all_to_all x1, waiting for transfers between devices, body(): lax.all_to_all(outgoing_rows, 'col', split_axis=0, concat_axis=0, tiled=T...  142 us
    all_to_all x1, waiting for transfers between devices, body(): lax.all_to_all(wanted_rows, 'col', split_axis=0, concat_axis=0, tiled=True)  139 us
    reduce_scatter x1, waiting for transfers between devices, body(): lax.psum_scatter(dense_rows.astype(jnp.bfloat16), 'row', scatter_dimensio...  43.4 us
    all_gather x1, waiting for transfers between devices, body(): column = lax.all_gather(projected, 'row', axis=0, tiled=True)  35.5 us
    all_to_all x1, blocking collectives, all_sum(): lax.all_to_all(packed.reshape(devices, chunk, width), ('row', 'col'), 0,...  34.6 us
    all_to_all x1, waiting for transfers between devices, all_sum(): lax.all_to_all(jnp.broadcast_to(owned[None], (devices, chunk, width)), ('...  20.3 us
    pallas_call x2, Pallas kernels, tile_sums(): pl.pallas_call(functools.partial(tile_kernel, transpose=transpose), out_s...  15.6 us
    all_to_all x1, starting transfers between devices, body(): lax.all_to_all(outgoing_rows, 'col', split_axis=0, concat_axis=0, tiled=T...  14.5 us
  transfers between devices with their start and end apart: 5, of which 5 were waited for; matrix products, arithmetic and copies ran while one was open for 1% of the time, Pallas kernels for 0%

profile of v3, /device:TPU:1, one launch (start us, length us, event | category | flops | bytes accessed | tf_op | source)
XLA Modules:
  0.0 510.3 jit_solution(6372351894344000161)
XLA Ops:
  7.2 0.0 copy-start
  7.2 0.0 all-gather.2.cloned.1.call-start
  7.2 1.0 copy-done
  8.2 2.0 convolution_convert_fusion.2
  10.2 0.0 all-gather.2.cloned.1.call-update
  10.2 0.7 maximum_add_fusion
  10.9 0.1 copy.19
  11.0 0.1 reshape.96
  11.8 0.7 compare_select_fusion.1
  12.4 1.3 gather_fusion
  13.7 35.5 %all-gather.2.cloned.1.call-done = bf16[8192,256]{1,0:T(8,128)(2,1)} async-done(((bf16[1024,256]{1,0:T(8,128)(2,1)}), bf16[8192,256]{1,0:T(8,128)(2,1)}) %all-gather.2.cloned.1.call-update) | async-done | bytes 4194320 | tf_op jit(solution)/shard_map/all_gather | solution.py:99
  49.2 8.4 %shard_map.129 = bf16[96,128,256]{2,1,0:T(8,128)(2,1)} custom-call(s32[48]{0:T(128)} %gather_fusion, s32[48]{0:T(128)} %take_ref.1, s32[1]{0:T(128)S(6)} %copy.24.count_ref, bf16[48,128,128]{2,1,0:T(8,128)(2,1)} %adj_ref.3, bf16[64,128,256]{2,1,0:T(8,128)(2,1)} %bitcast.30), custom_call_target="tpu_custom_call" | custom-call | flops 402653184 | bytes 12058624 | tf_op jit(solution)/shard_map/pallas_call | solution.py:44
  57.7 0.0 copy-start.2
  57.7 14.5 %all-to-all-start = ((bf16[32,3,128,256]{3,2,1,0:T(8,128)(2,1)}), bf16[32,3,128,256]{3,2,1,0:T(8,128)(2,1)}, u32[]{:S(2)}, u32[]{:S(2)}) async-start(bf16[32,3,128,256]{3,2,1,0:T(8,128)(2,1)} %bitcast.25), calls=%async_computation | async-start | bytes 12582912 | tf_op jit(solution)/shard_map/all_to_all | solution.py:117
  72.2 0.0 copy-done.2
  72.2 0.1 copy.18
  72.3 0.1 eq.28
  72.4 0.1 copy.21
  72.5 0.1 reshape.102
  72.6 142.1 %all-to-all-done = bf16[32,3,128,256]{3,2,1,0:T(8,128)(2,1)} async-done(((bf16[32,3,128,256]{3,2,1,0:T(8,128)(2,1)}), bf16[32,3,128,256]{3,2,1,0:T(8,128)(2,1)}, u32[]{:S(2)}, u32[]{:S(2)}) %all-to-all-start) | async-done | bytes 6291488 | tf_op jit(solution)/shard_map/all_to_all | solution.py:117
  214.8 6.9 %copy.22 = bf16[12,8,128,256]{3,1,2,0:T(8,128)(2,1)S(1)} copy(bf16[12,8,128,256]{3,2,1,0:T(8,128)(2,1)} %bitcast.10) | data formatting | bytes 12582912
  221.7 0.0 copy-start.4
  221.7 0.9 fusion.4
  222.6 0.2 reshape.100
  222.8 0.0 copy-done.4
  222.8 2.3 fusion.7
  225.1 5.9 %gather_fusion.1 = bf16[96,128,256]{2,1,0:T(8,128)(2,1)} fusion(bf16[8,128,256]{2,1,0:T(8,128)(2,1)S(1)} %bitcast.24, s32[1024]{0:T(1024)S(1)} %pad_clamp_fusion), kind=kCustom, calls=%fused_computation.1 | custom fusion | bytes 12583296 | tf_op jit(solution)/shard_map/gather | solution.py:131
  231.1 0.0 copy-start.3
  231.1 10.9 %all-to-all-start.1 = ((bf16[32,3,128,256]{3,2,1,0:T(8,128)(2,1)}), bf16[32,3,128,256]{3,2,1,0:T(8,128)(2,1)}, u32[]{:S(2)}, u32[]{:S(2)}) async-start(bf16[32,3,128,256]{3,2,1,0:T(8,128)(2,1)} %bitcast.26), calls=%async_computation.1 | async-start | bytes 12582912 | tf_op jit(solution)/shard_map/all_to_all | solution.py:134
  241.9 0.0 reduce-scatter.2.cloned.1.call-start
  242.0 0.0 copy-done.3
  242.0 0.1 copy.20
  242.1 0.1 ge.11
  242.2 138.5 %all-to-all-done.1 = bf16[32,3,128,256]{3,2,1,0:T(8,128)(2,1)} async-done(((bf16[32,3,128,256]{3,2,1,0:T(8,128)(2,1)}), bf16[32,3,128,256]{3,2,1,0:T(8,128)(2,1)}, u32[]{:S(2)}, u32[]{:S(2)}) %all-to-all-start.1) | async-done | bytes 6291488 | tf_op jit(solution)/shard_map/all_to_all | solution.py:134
  380.7 7.2 %shard_map.130 = bf16[24,128,256]{2,1,0:T(8,128)(2,1)} custom-call(s32[48]{0:T(128)} %take_ref.1, s32[48]{0:T(128)} %put_ref.3, s32[1]{0:T(128)S(6)} %copy.24.count_ref, bf16[48,128,128]{2,1,0:T(8,128)(2,1)} %adj_ref.3, bf16[96,128,256]{2,1,0:T(8,128)(2,1)} %bitcast.5.operand_ref), custom_call_target="tpu_custom_call" | custom-call | flops 402653184 | bytes 9437184 | tf_op jit(solution)/shard_map/pallas_call | solution.py:44
  387.9 2.3 copy.23
  390.2 3.2 convolution_convert_fusion
  393.4 0.0 copy-start.1
  393.4 0.0 reduce-scatter.2.cloned.1.call-update
  393.4 43.4 %reduce-scatter.2.cloned.1.call-done = bf16[8,32768]{1,0:T(8,128)(2,1)} async-done(((bf16[64,32768]{1,0:T(8,128)(2,1)}), bf16[8,32768]{1,0:T(8,128)(2,1)}) %reduce-scatter.2.cloned.1.call-update) | async-done | bytes 524304 | tf_op jit(solution)/shard_map/reduce_scatter | solution.py:147
  436.8 1.3 convert_element_type.32
  438.1 0.4 convolution_bitcast_fusion
  438.5 0.3 reshape.106
  438.8 34.6 %all_to_all.20 = f32[256,2,256]{2,1,0:T(2,128)S(1)} all-to-all(f32[256,2,256]{2,1,0:T(2,128)S(1)} %reshape.106), channel_id=1, replica_groups=mesh['row'=8,'col'=32] {'row','col'}, dimensions={0} | all-to-all | bytes 1048576 | tf_op jit(solution)/shard_map/all_to_all | solution.py:67
  473.4 0.3 reduce_sum.19
  473.7 0.9 broadcast_in_dim.8
  474.6 5.4 %all-to-all-start.3 = ((f32[256,2,256]{2,1,0:T(2,128)}), f32[256,2,256]{2,1,0:T(2,128)S(1)}, u32[]{:S(2)}, u32[]{:S(2)}) async-start(f32[256,2,256]{2,1,0:T(2,128)} %broadcast_in_dim.8), calls=%async_computation.4 | async-start | bytes 1048576 | tf_op jit(solution)/shard_map/all_to_all | solution.py:71
  480.1 0.0 copy-done.1
  480.1 1.1 convolution_convert_fusion.1
  481.2 20.3 %all-to-all-done.3 = f32[256,2,256]{2,1,0:T(2,128)S(1)} async-done(((f32[256,2,256]{2,1,0:T(2,128)}), f32[256,2,256]{2,1,0:T(2,128)S(1)}, u32[]{:S(2)}, u32[]{:S(2)}) %all-to-all-start.3) | async-done | bytes 524320 | tf_op jit(solution)/shard_map/all_to_all | solution.py:71
  501.5 0.4 reshape.107
  501.9 0.6 slice_multiply_fusion.1
  502.5 0.1 slice_multiply_fusion
  502.6 0.9 mul.46
  (7 shorter events, 0.1 us)
Async XLA Ops:
  7.2 1.0 copy-start
  7.2 42.0 %all-gather.2.cloned.1.call-start = ((), (), s32[]{:S(2)}) async-start(), calls=%async_computation.5 | async-start | bytes 4718592 | tf_op jit(solution)/shard_map/all_gather | solution.py:99
  57.7 14.5 %copy-start.2 = (s32[32,3]{0,1:T(4,128)S(1)}, s32[32,3]{0,1:T(4,128)}, u32[]{:S(2)}) copy-start(s32[32,3]{0,1:T(4,128)} %param.18) | copy-start | bytes 1156
  57.7 157.1 %all-to-all-start = ((bf16[32,3,128,256]{3,2,1,0:T(8,128)(2,1)}), bf16[32,3,128,256]{3,2,1,0:T(8,128)(2,1)}, u32[]{:S(2)}, u32[]{:S(2)}) async-start(bf16[32,3,128,256]{3,2,1,0:T(8,128)(2,1)} %bitcast.25), calls=%async_computation | async-start | bytes 12582912 | tf_op jit(solution)/shard_map/all_to_all | solution.py:117
  221.7 1.1 copy-start.4
  231.1 10.9 %copy-start.3 = (s32[8,3]{0,1:T(4,128)S(1)}, s32[8,3]{0,1:T(4,128)}, u32[]{:S(2)}) copy-start(s32[8,3]{0,1:T(4,128)} %param.17) | copy-start | bytes 292
  231.1 149.6 %all-to-all-start.1 = ((bf16[32,3,128,256]{3,2,1,0:T(8,128)(2,1)}), bf16[32,3,128,256]{3,2,1,0:T(8,128)(2,1)}, u32[]{:S(2)}, u32[]{:S(2)}) async-start(bf16[32,3,128,256]{3,2,1,0:T(8,128)(2,1)} %bitcast.26), calls=%async_computation.1 | async-start | bytes 12582912 | tf_op jit(solution)/shard_map/all_to_all | solution.py:134
  241.9 194.8 %reduce-scatter.2.cloned.1.call-start = ((), (), s32[]{:S(2)}) async-start(), calls=%async_computation.6 | async-start | bytes 4718592 | tf_op jit(solution)/shard_map/reduce_scatter | solution.py:147
  393.4 86.7 %copy-start.1 = (bf16[256,256]{1,0:T(8,128)(2,1)S(1)}, bf16[256,256]{1,0:T(8,128)(2,1)}, u32[]{:S(2)}) copy-start(bf16[256,256]{1,0:T(8,128)(2,1)} %param.11) | copy-start | bytes 393220
  474.6 26.9 %all-to-all-start.3 = ((f32[256,2,256]{2,1,0:T(2,128)}), f32[256,2,256]{2,1,0:T(2,128)S(1)}, u32[]{:S(2)}, u32[]{:S(2)}) async-start(f32[256,2,256]{2,1,0:T(2,128)} %broadcast_in_dim.8), calls=%async_computation.4 | async-start | bytes 1048576 | tf_op jit(solution)/shard_map/all_to_all | solution.py:71
Sparse Core Ops, SparseCore 0:
  10.4 38.7 all-gather.1
  393.5 43.2 reduce-scatter.1

commit v4 on v3

--- a/solution.py
+++ b/solution.py
@@ -95,8 +95,10 @@
     deliver_cap = deliver_list.shape[1]
     block_cells = tile_side * feat_width
     live_count = tile_count[0]
-    projected = jnp.dot(features, weight, preferred_element_type=jnp.float32).astype(jnp.bfloat16)
-    column = lax.all_gather(projected, "row", axis=0, tiled=True)
+    column_features = lax.all_gather(features, "row", axis=0, tiled=True)
+    column = jnp.dot(column_features, weight, preferred_element_type=jnp.float32).astype(
+        jnp.bfloat16
+    )
     source_operand = column.reshape(row_devices * own_blocks, tile_side, feat_width)
     global_ids = (
         jnp.arange(row_devices, dtype=jnp.int32)[:, None] * own_blocks + jnp.maximum(fetch_list, 0)
@@ -143,18 +145,21 @@
         (global_ids[None, :] == jnp.arange(row_devices * own_blocks, dtype=jnp.int32)[:, None])
         & valid_slots[None, :]
     ).astype(jnp.bfloat16)
-    dense_rows = jnp.dot(onehot, rounded, preferred_element_type=jnp.float32)
+    dense_rows = jnp.dot(onehot, rounded, preferred_element_type=jnp.float32).astype(jnp.bfloat16)
+    weight_term = lax.dot_general(
+        column_features,
+        dense_rows.reshape(row_devices * node_rows, feat_width),
+        (((0,), (0,)), ((), ())),
+        preferred_element_type=jnp.float32,
+    )
+    grad_weight, grad_bias = all_sum(weight_term, bias_term)
     owned_sums = lax.psum_scatter(
-        dense_rows.astype(jnp.bfloat16), "row", scatter_dimension=0, tiled=True
+        dense_rows, "row", scatter_dimension=0, tiled=True
     ).astype(jnp.float32)
     grad_proj = owned_sums.reshape(node_rows, feat_width).astype(jnp.bfloat16)
     grad_features = jnp.dot(grad_proj, weight.T, preferred_element_type=jnp.float32).astype(
         jnp.bfloat16
     )
-    weight_term = lax.dot_general(
-        features, grad_proj, (((0,), (0,)), ((), ())), preferred_element_type=jnp.float32
-    )
-    grad_weight, grad_bias = all_sum(weight_term, bias_term)
     grad_scale = 1.0 / math.sqrt(node_rows * row_devices * col_devices)
     return (layer_out, grad_features, grad_weight * grad_scale, grad_bias * grad_scale)
 

time: 514 us -> 490 us (0.953)
  waiting for transfers between devices: 380 us -> 317 us
  blocking collectives: 34.6 us -> 60.8 us
  starting transfers between devices: 30.8 us -> 18.9 us
  Pallas kernels: 15.6 us -> 24.9 us
  matrix products: 7.58 us -> 15.9 us
  local copies, waits for them, and re-layouts: 22.1 us -> 27.8 us
    reduce_scatter x1, waiting for transfers between devices: 43.4 us -> 0.01 us  [body(): lax.psum_scatter(dense_rows, 'row', scatter_dimension=0, tiled=True)]
    all_to_all x0 -> x1, blocking collectives: none -> 26.6 us  [all_sum(): lax.all_to_all(jnp.broadcast_to(owned[None], (devices, chunk, width)), ('...]
    all_to_all x1 -> x0, waiting for transfers between devices: 20.3 us -> none  [all_sum(): lax.all_to_all(jnp.broadcast_to(owned[None], (devices, chunk, width)), ('...]
    pallas_call x2, Pallas kernels: 15.6 us -> 24.9 us  [tile_sums(): pl.pallas_call(functools.partial(tile_kernel, transpose=transpose), out_s...]
    dot_general x3, matrix products: 5.53 us -> 13.8 us  [the longest x1 5.45 us: body(): jnp.dot(column_features, weight, preferred_element_type=jnp.float32)]
    reshape x0 -> x1, local copies, waits for them, and re-layouts: none -> 7.43 us  [body(): dense_rows.reshape(row_devices * node_rows, feat_width)]
    all_to_all x1, starting transfers between devices: 14.5 us -> 8.59 us  [body(): lax.all_to_all(outgoing_rows, 'col', split_axis=0, concat_axis=0, tiled=T...]
    all_to_all x1 -> x0, starting transfers between devices: 5.4 us -> none  [all_sum(): lax.all_to_all(jnp.broadcast_to(owned[None], (devices, chunk, width)), ('...]
  transfers between devices with their start and end apart: 5 -> 4, of which waited for: 5 -> 3; matrix products, arithmetic and copies ran while one was open for 1% -> 4% of each run, Pallas kernels for 0% -> 0%
where the time goes in v4:
time: 490 us; the launch traced here: 483 us
  waiting for transfers between devices  317 us (65%)
  blocking collectives  60.8 us (12%)
  local copies, waits for them, and re-layouts  27.8 us (6%)
  Pallas kernels  24.9 us (5%)
  starting transfers between devices  18.9 us (4%)
  matrix products  15.9 us (3%)
  between operations  14.9 us (3%)
    all_to_all x1, waiting for transfers between devices, body(): lax.all_to_all(wanted_rows, 'col', split_axis=0, concat_axis=0, tiled=True)  140 us
    all_to_all x1, waiting for transfers between devices, body(): lax.all_to_all(outgoing_rows, 'col', split_axis=0, concat_axis=0, tiled=T...  139 us
    all_gather x1, waiting for transfers between devices, body(): column_features = lax.all_gather(features, 'row', axis=0, tiled=True)  37.3 us
    all_to_all x1, blocking collectives, all_sum(): lax.all_to_all(packed.reshape(devices, chunk, width), ('row', 'col'), 0,...  34.2 us
    all_to_all x1, blocking collectives, all_sum(): lax.all_to_all(jnp.broadcast_to(owned[None], (devices, chunk, width)), ('...  26.6 us
    pallas_call x2, Pallas kernels, tile_sums(): pl.pallas_call(functools.partial(tile_kernel, transpose=transpose), out_s...  24.9 us
    all_to_all x1, starting transfers between devices, body(): lax.all_to_all(wanted_rows, 'col', split_axis=0, concat_axis=0, tiled=True)  10 us
  transfers between devices with their start and end apart: 4, of which 3 were waited for; matrix products, arithmetic and copies ran while one was open for 4% of the time, Pallas kernels for 0%

profile of v4, /device:TPU:1, one launch (start us, length us, event | category | flops | bytes accessed | tf_op | source)
XLA Modules:
  0.0 483.4 jit_solution(14355628515590397014)
XLA Ops:
  7.2 0.0 copy-start
  7.2 0.0 all-gather.2.cloned.1.call-start
  7.2 0.7 all-gather.2.cloned.1.call-update
  7.9 0.7 maximum_add_fusion
  8.6 0.1 copy.19
  8.7 0.1 reshape.99
  9.4 0.7 compare_select_fusion.1
  10.1 1.3 gather_fusion
  11.4 37.3 %all-gather.2.cloned.1.call-done = bf16[8192,256]{1,0:T(8,128)(2,1)} async-done(((bf16[1024,256]{1,0:T(8,128)(2,1)}), bf16[8192,256]{1,0:T(8,128)(2,1)}) %all-gather.2.cloned.1.call-update) | async-done | bytes 4194320 | tf_op jit(solution)/shard_map/all_gather | solution.py:98
  48.6 0.0 copy-done
  48.6 5.5 %convolution_convert_fusion.1 = bf16[8192,256]{1,0:T(8,128)(2,1)} fusion(bf16[8192,256]{1,0:T(8,128)(2,1)} %all-gather.2.cloned.1.call-done, bf16[256,256]{1,0:T(8,128)(2,1)S(1)} %copy-done), kind=kOutput, calls=%fused_computation.3 | convolution fusion | flops 1075838976 | bytes 8519680 | tf_op jit(solution)/shard_map/dot_general | solution.py:99
  54.1 12.5 %shard_map.129 = bf16[96,128,256]{2,1,0:T(8,128)(2,1)} custom-call(s32[48]{0:T(128)} %gather_fusion, s32[48]{0:T(128)} %take_ref.1, s32[1]{0:T(128)S(6)} %copy.24.count_ref, bf16[48,128,128]{2,1,0:T(8,128)(2,1)} %adj_ref.3, bf16[64,128,256]{2,1,0:T(8,128)(2,1)} %bitcast.28), custom_call_target="tpu_custom_call" | custom-call | flops 402653184 | bytes 12058624 | tf_op jit(solution)/shard_map/pallas_call | solution.py:44
  66.6 0.0 copy-start.2
  66.6 8.6 %all-to-all-start = ((bf16[32,3,128,256]{3,2,1,0:T(8,128)(2,1)}), bf16[32,3,128,256]{3,2,1,0:T(8,128)(2,1)}, u32[]{:S(2)}, u32[]{:S(2)}) async-start(bf16[32,3,128,256]{3,2,1,0:T(8,128)(2,1)} %bitcast.25), calls=%async_computation | async-start | bytes 12582912 | tf_op jit(solution)/shard_map/all_to_all | solution.py:119
  75.2 0.0 copy-done.2
  75.2 0.1 copy.18
  75.3 0.1 eq.28
  75.4 0.1 copy.21
  75.5 0.1 reshape.105
  75.7 138.9 %all-to-all-done = bf16[32,3,128,256]{3,2,1,0:T(8,128)(2,1)} async-done(((bf16[32,3,128,256]{3,2,1,0:T(8,128)(2,1)}), bf16[32,3,128,256]{3,2,1,0:T(8,128)(2,1)}, u32[]{:S(2)}, u32[]{:S(2)}) %all-to-all-start) | async-done | bytes 6291488 | tf_op jit(solution)/shard_map/all_to_all | solution.py:119
  214.6 6.9 %copy.22 = bf16[12,8,128,256]{3,1,2,0:T(8,128)(2,1)S(1)} copy(bf16[12,8,128,256]{3,2,1,0:T(8,128)(2,1)} %bitcast.10) | data formatting | bytes 12582912
  221.5 0.0 copy-start.1
  221.5 0.0 copy-start.4
  221.5 0.9 fusion.4
  222.4 0.2 reshape.103
  222.6 0.0 copy-done.1
  222.6 0.0 copy-done.4
  222.6 1.3 fusion.7
  223.9 5.9 %gather_fusion.1 = bf16[96,128,256]{2,1,0:T(8,128)(2,1)} fusion(bf16[8,128,256]{2,1,0:T(8,128)(2,1)S(1)} %bitcast.24, s32[1024]{0:T(1024)S(1)} %pad_clamp_fusion), kind=kCustom, calls=%fused_computation.1 | custom fusion | bytes 12583296 | tf_op jit(solution)/shard_map/gather | solution.py:133
  229.9 0.0 copy-start.3
  229.9 10.0 %all-to-all-start.1 = ((bf16[32,3,128,256]{3,2,1,0:T(8,128)(2,1)}), bf16[32,3,128,256]{3,2,1,0:T(8,128)(2,1)}, u32[]{:S(2)}, u32[]{:S(2)}) async-start(bf16[32,3,128,256]{3,2,1,0:T(8,128)(2,1)} %bitcast.26), calls=%async_computation.1 | async-start | bytes 12582912 | tf_op jit(solution)/shard_map/all_to_all | solution.py:136
  239.9 0.2 reduce-scatter.2.cloned.1.call-start
  240.1 0.0 copy-done.3
  240.2 0.1 copy.20
  240.2 0.1 ge.11
  240.3 139.8 %all-to-all-done.1 = bf16[32,3,128,256]{3,2,1,0:T(8,128)(2,1)} async-done(((bf16[32,3,128,256]{3,2,1,0:T(8,128)(2,1)}), bf16[32,3,128,256]{3,2,1,0:T(8,128)(2,1)}, u32[]{:S(2)}, u32[]{:S(2)}) %all-to-all-start.1) | async-done | bytes 6291488 | tf_op jit(solution)/shard_map/all_to_all | solution.py:136
  380.2 12.4 %shard_map.130 = bf16[24,128,256]{2,1,0:T(8,128)(2,1)} custom-call(s32[48]{0:T(128)} %take_ref.1, s32[48]{0:T(128)} %put_ref.3, s32[1]{0:T(128)S(6)} %copy.24.count_ref, bf16[48,128,128]{2,1,0:T(8,128)(2,1)} %adj_ref.3, bf16[96,128,256]{2,1,0:T(8,128)(2,1)} %bitcast.5.operand_ref), custom_call_target="tpu_custom_call" | custom-call | flops 402653184 | bytes 9437184 | tf_op jit(solution)/shard_map/pallas_call | solution.py:44
  392.5 2.3 copy.23
  394.8 3.2 convolution_convert_fusion
  398.0 0.0 reduce-scatter.2.cloned.1.call-update
  398.0 7.4 %reshape.109 = bf16[8192,256]{1,0:T(8,128)(2,1)} reshape(bf16[64,32768]{1,0:T(8,128)(2,1)} %convolution_convert_fusion) | data formatting | bytes 8388608 | tf_op jit(solution)/shard_map/reshape | solution.py:151
  405.5 5.2 %convolution_bitcast_fusion = f32[256,256]{1,0:T(8,128)S(1)} fusion(bf16[8192,256]{1,0:T(8,128)(2,1)} %reshape.109, bf16[8192,256]{1,0:T(8,128)(2,1)} %all-gather.2.cloned.1.call-done), kind=kOutput, calls=%fused_computation.5 | convolution fusion | flops 1073741824 | bytes 8650752 | tf_op jit(solution)/shard_map/dot_general | solution.py:149
  410.7 0.3 reshape.110
  411.0 34.2 %all_to_all.20 = f32[256,2,256]{2,1,0:T(2,128)S(1)} all-to-all(f32[256,2,256]{2,1,0:T(2,128)S(1)} %reshape.110), channel_id=1, replica_groups=mesh['row'=8,'col'=32] {'row','col'}, dimensions={0} | all-to-all | bytes 1048576 | tf_op jit(solution)/shard_map/all_to_all | solution.py:67
  445.2 0.3 reduce_sum.19
  445.5 0.1 broadcast_in_dim.8
  445.7 26.6 %all_to_all.21 = f32[256,2,256]{2,1,0:T(2,128)S(1)} all-to-all(f32[256,2,256]{2,1,0:T(2,128)S(1)} %broadcast_in_dim.8), channel_id=1, replica_groups=mesh['row'=8,'col'=32] {'row','col'}, dimensions={0} | all-to-all | bytes 1048576 | tf_op jit(solution)/shard_map/all_to_all | solution.py:71
  472.2 0.1 slice_multiply_fusion
  472.4 0.9 mul.46
  473.2 0.4 reshape.111
  473.6 0.6 slice_multiply_fusion.1
  474.2 0.0 reduce-scatter.2.cloned.1.call-done
  474.2 1.3 convert_element_type.32
  475.5 1.1 convolution_convert_fusion.2
  (7 shorter events, 0.1 us)
Async XLA Ops:
  7.2 41.5 %copy-start = (bf16[256,256]{1,0:T(8,128)(2,1)S(1)}, bf16[256,256]{1,0:T(8,128)(2,1)}, u32[]{:S(2)}) copy-start(bf16[256,256]{1,0:T(8,128)(2,1)} %param.11) | copy-start | bytes 393220
  7.2 41.5 %all-gather.2.cloned.1.call-start = ((), (), s32[]{:S(2)}) async-start(), calls=%async_computation.5 | async-start | bytes 4718592 | tf_op jit(solution)/shard_map/all_gather | solution.py:98
  66.6 8.6 %copy-start.2 = (s32[32,3]{0,1:T(4,128)S(1)}, s32[32,3]{0,1:T(4,128)}, u32[]{:S(2)}) copy-start(s32[32,3]{0,1:T(4,128)} %param.18) | copy-start | bytes 1156
  66.6 147.9 %all-to-all-start = ((bf16[32,3,128,256]{3,2,1,0:T(8,128)(2,1)}), bf16[32,3,128,256]{3,2,1,0:T(8,128)(2,1)}, u32[]{:S(2)}, u32[]{:S(2)}) async-start(bf16[32,3,128,256]{3,2,1,0:T(8,128)(2,1)} %bitcast.25), calls=%async_computation | async-start | bytes 12582912 | tf_op jit(solution)/shard_map/all_to_all | solution.py:119
  221.5 1.1 copy-start.1
  221.5 1.1 copy-start.4
  229.9 10.2 %copy-start.3 = (s32[8,3]{0,1:T(4,128)S(1)}, s32[8,3]{0,1:T(4,128)}, u32[]{:S(2)}) copy-start(s32[8,3]{0,1:T(4,128)} %param.17) | copy-start | bytes 292
  229.9 150.3 %all-to-all-start.1 = ((bf16[32,3,128,256]{3,2,1,0:T(8,128)(2,1)}), bf16[32,3,128,256]{3,2,1,0:T(8,128)(2,1)}, u32[]{:S(2)}, u32[]{:S(2)}) async-start(bf16[32,3,128,256]{3,2,1,0:T(8,128)(2,1)} %bitcast.26), calls=%async_computation.1 | async-start | bytes 12582912 | tf_op jit(solution)/shard_map/all_to_all | solution.py:136
  239.9 234.3 %reduce-scatter.2.cloned.1.call-start = ((), (), s32[]{:S(2)}) async-start(), calls=%async_computation.6 | async-start | bytes 4718592 | tf_op jit(solution)/shard_map/reduce_scatter | solution.py:156
Sparse Core Ops, SparseCore 0:
  9.8 38.7 all-gather.1
  398.2 42.5 reduce-scatter.1

commit v5 on v4

--- a/solution.py
+++ b/solution.py
@@ -95,7 +95,13 @@
     deliver_cap = deliver_list.shape[1]
     block_cells = tile_side * feat_width
     live_count = tile_count[0]
-    column_features = lax.all_gather(features, "row", axis=0, tiled=True)
+    column_features = lax.all_to_all(
+        jnp.broadcast_to(features[None], (row_devices, node_rows, feat_width)),
+        "row",
+        0,
+        0,
+        tiled=True,
+    ).reshape(row_devices * node_rows, feat_width)
     column = jnp.dot(column_features, weight, preferred_element_type=jnp.float32).astype(
         jnp.bfloat16
     )
@@ -153,9 +159,16 @@
         preferred_element_type=jnp.float32,
     )
     grad_weight, grad_bias = all_sum(weight_term, bias_term)
-    owned_sums = lax.psum_scatter(
-        dense_rows, "row", scatter_dimension=0, tiled=True
-    ).astype(jnp.float32)
+    owned_sums = jnp.sum(
+        lax.all_to_all(
+            dense_rows.reshape(row_devices, own_blocks, tile_side, feat_width),
+            "row",
+            0,
+            0,
+            tiled=True,
+        ).astype(jnp.float32),
+        axis=0,
+    )
     grad_proj = owned_sums.reshape(node_rows, feat_width).astype(jnp.bfloat16)
     grad_features = jnp.dot(grad_proj, weight.T, preferred_element_type=jnp.float32).astype(
         jnp.bfloat16

time: 490 us -> 543 us (1.11); the launches traced: 483 us -> 543 us
  waiting for transfers between devices: 317 us -> 376 us
  starting transfers between devices: 18.9 us -> 36.9 us
  between operations: 14.9 us -> 1.49 us
  Pallas kernels: 24.9 us -> 15.8 us
    all_to_all x0 -> x2, waiting for transfers between devices: none -> 93.5 us  [the longest x1 46.9 us: body(): lax.all_to_all(dense_rows.reshape(row_devices, own_blocks, tile_side, fea...]
    all_gather x1 -> x0, waiting for transfers between devices: 37.3 us -> none  [body(): column_features = lax.all_gather(features, 'row', axis=0, tiled=True)]
    all_to_all x0 -> x2, starting transfers between devices: none -> 12.6 us  [the longest x1 7.77 us: body(): lax.all_to_all(jnp.broadcast_to(features[None], (row_devices, node_rows,...]
    pallas_call x2, Pallas kernels: 24.9 us -> 15.8 us  [tile_sums(): pl.pallas_call(functools.partial(tile_kernel, transpose=transpose), out_s...]
  transfers between devices with their start and end apart: 4 -> 4, of which waited for: 3 -> 4; matrix products, arithmetic and copies ran while one was open for 4% -> 1% of each run, Pallas kernels for 0% -> 0%
where the time goes in v5:
time: 543 us
  waiting for transfers between devices  376 us (69%)
  blocking collectives  62.4 us (11%)
  starting transfers between devices  36.9 us (7%)
  local copies, waits for them, and re-layouts  29.9 us (6%)
  matrix products  15.9 us (3%)
  Pallas kernels  15.8 us (3%)
    all_to_all x1, waiting for transfers between devices, body(): lax.all_to_all(outgoing_rows, 'col', split_axis=0, concat_axis=0, tiled=T...  143 us
    all_to_all x1, waiting for transfers between devices, body(): lax.all_to_all(wanted_rows, 'col', split_axis=0, concat_axis=0, tiled=True)  139 us
    all_to_all x1, waiting for transfers between devices, body(): lax.all_to_all(dense_rows.reshape(row_devices, own_blocks, tile_side, fea...  46.9 us
    all_to_all x1, waiting for transfers between devices, body(): lax.all_to_all(jnp.broadcast_to(features[None], (row_devices, node_rows,...  46.6 us
    all_to_all x1, blocking collectives, all_sum(): lax.all_to_all(packed.reshape(devices, chunk, width), ('row', 'col'), 0,...  35.8 us
    all_to_all x1, blocking collectives, all_sum(): lax.all_to_all(jnp.broadcast_to(owned[None], (devices, chunk, width)), ('...  26.6 us
    pallas_call x2, Pallas kernels, tile_sums(): pl.pallas_call(functools.partial(tile_kernel, transpose=transpose), out_s...  15.8 us
    all_to_all x1, starting transfers between devices, body(): lax.all_to_all(outgoing_rows, 'col', split_axis=0, concat_axis=0, tiled=T...  14 us
  transfers between devices with their start and end apart: 4, of which 4 were waited for; matrix products, arithmetic and copies ran while one was open for 1% of the time, Pallas kernels for 0%

profile of v5, /device:TPU:1, one launch (start us, length us, event | category | flops | bytes accessed | tf_op | source)
XLA Modules:
  0.0 543.4 jit_solution(3482530203070320583)
XLA Ops:
  0.6 0.0 copy-start
  0.6 3.3 broadcast_in_dim.9
  3.9 0.0 copy-start.3
  3.9 0.0 copy-start.5
  3.9 7.8 %all-to-all-start = ((bf16[8,1024,256]{2,1,0:T(8,128)(2,1)}), bf16[8,1024,256]{2,1,0:T(8,128)(2,1)}, u32[]{:S(2)}, u32[]{:S(2)}) async-start(bf16[8,1024,256]{2,1,0:T(8,128)(2,1)} %broadcast_in_dim.9), calls=%async_computation | async-start | bytes 8388608 | tf_op jit(solution)/shard_map/all_to_all | solution.py:98
  11.7 0.0 copy-done.3
  11.7 0.1 copy.27
  11.8 0.1 reshape.106
  12.6 0.0 copy-done.5
  12.6 1.3 gather_fusion
  13.9 46.6 %all-to-all-done = bf16[8,1024,256]{2,1,0:T(8,128)(2,1)} async-done(((bf16[8,1024,256]{2,1,0:T(8,128)(2,1)}), bf16[8,1024,256]{2,1,0:T(8,128)(2,1)}, u32[]{:S(2)}, u32[]{:S(2)}) %all-to-all-start) | async-done | bytes 4194336 | tf_op jit(solution)/shard_map/all_to_all | solution.py:98
  60.5 0.0 copy-done
  60.5 5.5 %convolution_convert_fusion.1 = bf16[8192,256]{1,0:T(8,128)(2,1)} fusion(bf16[8192,256]{1,0:T(8,128)(2,1)} %bitcast, bf16[256,256]{1,0:T(8,128)(2,1)S(1)} %copy-done), kind=kOutput, calls=%fused_computation.3 | convolution fusion | flops 1075838976 | bytes 8519680 | tf_op jit(solution)/shard_map/dot_general | solution.py:105
  66.0 8.6 %shard_map.129 = bf16[96,128,256]{2,1,0:T(8,128)(2,1)} custom-call(s32[48]{0:T(128)} %gather_fusion, s32[48]{0:T(128)} %take_ref.1, s32[1]{0:T(128)S(6)} %copy.33.count_ref, bf16[48,128,128]{2,1,0:T(8,128)(2,1)} %adj_ref.3, bf16[64,128,256]{2,1,0:T(8,128)(2,1)} %bitcast.32), custom_call_target="tpu_custom_call" | custom-call | flops 402653184 | bytes 12058624 | tf_op jit(solution)/shard_map/pallas_call | solution.py:44
  74.6 0.0 copy-start.2
  74.6 14.0 %all-to-all-start.1 = ((bf16[32,3,128,256]{3,2,1,0:T(8,128)(2,1)}), bf16[32,3,128,256]{3,2,1,0:T(8,128)(2,1)}, u32[]{:S(2)}, u32[]{:S(2)}) async-start(bf16[32,3,128,256]{3,2,1,0:T(8,128)(2,1)} %bitcast.29), calls=%async_computation.1 | async-start | bytes 12582912 | tf_op jit(solution)/shard_map/all_to_all | solution.py:125
  88.6 0.0 copy-done.2
  88.6 0.1 copy.26
  88.7 0.1 eq.28
  88.8 0.1 copy.29
  88.9 0.1 reshape.113
  89.0 143.3 %all-to-all-done.1 = bf16[32,3,128,256]{3,2,1,0:T(8,128)(2,1)} async-done(((bf16[32,3,128,256]{3,2,1,0:T(8,128)(2,1)}), bf16[32,3,128,256]{3,2,1,0:T(8,128)(2,1)}, u32[]{:S(2)}, u32[]{:S(2)}) %all-to-all-start.1) | async-done | bytes 6291488 | tf_op jit(solution)/shard_map/all_to_all | solution.py:125
  232.2 6.9 %copy.31 = bf16[12,8,128,256]{3,1,2,0:T(8,128)(2,1)S(1)} copy(bf16[12,8,128,256]{3,2,1,0:T(8,128)(2,1)} %bitcast.13) | data formatting | bytes 12582912
  239.2 0.0 copy-start.1
  239.2 0.0 copy-start.4
  239.2 0.9 fusion.4
  240.1 0.2 reshape.111
  240.3 0.0 copy-done.1
  240.3 0.0 copy-done.4
  240.3 1.3 fusion.7
  241.6 5.9 %gather_fusion.1 = bf16[96,128,256]{2,1,0:T(8,128)(2,1)} fusion(bf16[8,128,256]{2,1,0:T(8,128)(2,1)S(1)} %bitcast.27, s32[1024]{0:T(1024)S(1)} %pad_clamp_fusion), kind=kCustom, calls=%fused_computation.1 | custom fusion | bytes 12583296 | tf_op jit(solution)/shard_map/gather | solution.py:139
  247.6 10.3 %all-to-all-start.2 = ((bf16[32,3,128,256]{3,2,1,0:T(8,128)(2,1)}), bf16[32,3,128,256]{3,2,1,0:T(8,128)(2,1)}, u32[]{:S(2)}, u32[]{:S(2)}) async-start(bf16[32,3,128,256]{3,2,1,0:T(8,128)(2,1)} %bitcast.30), calls=%async_computation.2 | async-start | bytes 12582912 | tf_op jit(solution)/shard_map/all_to_all | solution.py:142
  257.9 0.1 copy.28
  258.0 0.1 ge.11
  258.1 138.9 %all-to-all-done.2 = bf16[32,3,128,256]{3,2,1,0:T(8,128)(2,1)} async-done(((bf16[32,3,128,256]{3,2,1,0:T(8,128)(2,1)}), bf16[32,3,128,256]{3,2,1,0:T(8,128)(2,1)}, u32[]{:S(2)}, u32[]{:S(2)}) %all-to-all-start.2) | async-done | bytes 6291488 | tf_op jit(solution)/shard_map/all_to_all | solution.py:142
  397.0 7.2 %shard_map.130 = bf16[24,128,256]{2,1,0:T(8,128)(2,1)} custom-call(s32[48]{0:T(128)} %take_ref.1, s32[48]{0:T(128)} %put_ref.3, s32[1]{0:T(128)S(6)} %copy.33.count_ref, bf16[48,128,128]{2,1,0:T(8,128)(2,1)} %adj_ref.3, bf16[96,128,256]{2,1,0:T(8,128)(2,1)} %bitcast.6.operand_ref), custom_call_target="tpu_custom_call" | custom-call | flops 402653184 | bytes 9437184 | tf_op jit(solution)/shard_map/pallas_call | solution.py:44
  404.2 2.3 copy.32
  406.5 3.2 convolution_convert_fusion
  409.7 7.4 %reshape.118 = bf16[8192,256]{1,0:T(8,128)(2,1)} reshape(bf16[64,32768]{1,0:T(8,128)(2,1)} %convolution_convert_fusion) | data formatting | bytes 8388608 | tf_op jit(solution)/shard_map/reshape | solution.py:157
  417.1 5.2 convolution_bitcast_fusion
  422.4 0.3 reshape.119
  422.7 35.8 %all_to_all.30 = f32[256,2,256]{2,1,0:T(2,128)S(1)} all-to-all(f32[256,2,256]{2,1,0:T(2,128)S(1)} %reshape.119), channel_id=1, replica_groups=mesh['row'=8,'col'=32] {'row','col'}, dimensions={0} | all-to-all | bytes 1048576 | tf_op jit(solution)/shard_map/all_to_all | solution.py:67
  458.4 0.3 reduce_sum.32
  458.7 0.1 broadcast_in_dim.11
  458.9 26.6 %all_to_all.31 = f32[256,2,256]{2,1,0:T(2,128)S(1)} all-to-all(f32[256,2,256]{2,1,0:T(2,128)S(1)} %broadcast_in_dim.11), channel_id=1, replica_groups=mesh['row'=8,'col'=32] {'row','col'}, dimensions={0} | all-to-all | bytes 1048576 | tf_op jit(solution)/shard_map/all_to_all | solution.py:71
  485.5 4.8 all-to-all-start.3
  490.3 0.1 slice_multiply_fusion
  490.4 0.9 mul.46
  491.3 0.4 reshape.120
  491.6 0.6 slice_multiply_fusion.1
  492.2 46.9 %all-to-all-done.3 = bf16[8,8,128,256]{3,1,2,0:T(8,128)(2,1)} async-done(((bf16[8,8,128,256]{3,1,2,0:T(8,128)(2,1)}), bf16[8,8,128,256]{3,1,2,0:T(8,128)(2,1)}, u32[]{:S(2)}, u32[]{:S(2)}) %all-to-all-start.3) | async-done | bytes 4194336 | tf_op jit(solution)/shard_map/all_to_all | solution.py:163
  539.1 3.0 reduce_sum.30
  542.1 0.1 copy.30
  542.3 1.1 convolution_convert_fusion.2
  (9 shorter events, 0.1 us)
Async XLA Ops:
  0.6 59.9 %copy-start = (bf16[256,256]{1,0:T(8,128)(2,1)S(1)}, bf16[256,256]{1,0:T(8,128)(2,1)}, u32[]{:S(2)}) copy-start(bf16[256,256]{1,0:T(8,128)(2,1)} %param.11) | copy-start | bytes 393220
  3.9 7.8 %copy-start.3 = (s32[8,3]{0,1:T(4,128)S(1)}, s32[8,3]{0,1:T(4,128)}, u32[]{:S(2)}) copy-start(s32[8,3]{0,1:T(4,128)} %param.17) | copy-start | bytes 292
  3.9 8.6 %copy-start.5 = (s32[48]{0:T(128)S(1)}, s32[48]{0:T(128)}, u32[]{:S(2)}) copy-start(s32[48]{0:T(128)} %put_ref.3) | copy-start | bytes 580
  3.9 56.6 %all-to-all-start = ((bf16[8,1024,256]{2,1,0:T(8,128)(2,1)}), bf16[8,1024,256]{2,1,0:T(8,128)(2,1)}, u32[]{:S(2)}, u32[]{:S(2)}) async-start(bf16[8,1024,256]{2,1,0:T(8,128)(2,1)} %broadcast_in_dim.9), calls=%async_computation | async-start | bytes 8388608 | tf_op jit(solution)/shard_map/all_to_all | solution.py:98
  74.6 14.0 %copy-start.2 = (s32[32,3]{0,1:T(4,128)S(1)}, s32[32,3]{0,1:T(4,128)}, u32[]{:S(2)}) copy-start(s32[32,3]{0,1:T(4,128)} %param.18) | copy-start | bytes 1156
  74.6 157.7 %all-to-all-start.1 = ((bf16[32,3,128,256]{3,2,1,0:T(8,128)(2,1)}), bf16[32,3,128,256]{3,2,1,0:T(8,128)(2,1)}, u32[]{:S(2)}, u32[]{:S(2)}) async-start(bf16[32,3,128,256]{3,2,1,0:T(8,128)(2,1)} %bitcast.29), calls=%async_computation.1 | async-start | bytes 12582912 | tf_op jit(solution)/shard_map/all_to_all | solution.py:125
  239.2 1.1 copy-start.1
  239.2 1.1 copy-start.4
  247.6 149.4 %all-to-all-start.2 = ((bf16[32,3,128,256]{3,2,1,0:T(8,128)(2,1)}), bf16[32,3,128,256]{3,2,1,0:T(8,128)(2,1)}, u32[]{:S(2)}, u32[]{:S(2)}) async-start(bf16[32,3,128,256]{3,2,1,0:T(8,128)(2,1)} %bitcast.30), calls=%async_computation.2 | async-start | bytes 12582912 | tf_op jit(solution)/shard_map/all_to_all | solution.py:142
  485.5 53.6 %all-to-all-start.3 = ((bf16[8,8,128,256]{3,1,2,0:T(8,128)(2,1)}), bf16[8,8,128,256]{3,1,2,0:T(8,128)(2,1)}, u32[]{:S(2)}, u32[]{:S(2)}) async-start(bf16[8,8,128,256]{3,1,2,0:T(8,128)(2,1)} %bitcast.28), calls=%async_computation.3 | async-start | bytes 8388608 | tf_op jit(solution)/shard_map/all_to_all | solution.py:163

commit v6 on v4

--- a/solution.py
+++ b/solution.py
@@ -146,9 +146,12 @@
         & valid_slots[None, :]
     ).astype(jnp.bfloat16)
     dense_rows = jnp.dot(onehot, rounded, preferred_element_type=jnp.float32).astype(jnp.bfloat16)
+    slot_features = column_features.reshape(row_devices * own_blocks, tile_side, feat_width)[
+        global_ids
+    ]
     weight_term = lax.dot_general(
-        column_features,
-        dense_rows.reshape(row_devices * node_rows, feat_width),
+        slot_features.reshape(row_devices * fetch_cap * tile_side, feat_width),
+        src_sums.reshape(row_devices * fetch_cap * tile_side, feat_width),
         (((0,), (0,)), ((), ())),
         preferred_element_type=jnp.float32,
     )

time: 490 us -> 482 us (0.984); the launches traced: 483 us -> 482 us
  blocking collectives: 60.8 us -> 74.6 us
  Pallas kernels: 24.9 us -> 19.3 us
    all_to_all x1, blocking collectives: 34.2 us -> 48.1 us  [all_sum(): lax.all_to_all(packed.reshape(devices, chunk, width), ('row', 'col'), 0,...]
    reshape x1 -> x0, local copies, waits for them, and re-layouts: 7.43 us -> none  [body(): dense_rows.reshape(row_devices * node_rows, feat_width)]
    pallas_call x2, Pallas kernels: 24.9 us -> 19.3 us  [tile_sums(): pl.pallas_call(functools.partial(tile_kernel, transpose=transpose), out_s...]
  transfers between devices with their start and end apart: 4 -> 4, of which waited for: 3 -> 3; matrix products, arithmetic and copies ran while one was open for 4% -> 2% of each run, Pallas kernels for 0% -> 0%
where the time goes in v6:
time: 482 us
  waiting for transfers between devices  315 us (65%)
  blocking collectives  74.6 us (15%)
  local copies, waits for them, and re-layouts  23.4 us (5%)
  starting transfers between devices  20.2 us (4%)
  Pallas kernels  19.3 us (4%)
  between operations  14.9 us (3%)
  matrix products  11.3 us (2%)
    all_to_all x1, waiting for transfers between devices, body(): lax.all_to_all(wanted_rows, 'col', split_axis=0, concat_axis=0, tiled=True)  139 us
    all_to_all x1, waiting for transfers between devices, body(): lax.all_to_all(outgoing_rows, 'col', split_axis=0, concat_axis=0, tiled=T...  138 us
    all_to_all x1, blocking collectives, all_sum(): lax.all_to_all(packed.reshape(devices, chunk, width), ('row', 'col'), 0,...  48.1 us
    all_gather x1, waiting for transfers between devices, body(): column_features = lax.all_gather(features, 'row', axis=0, tiled=True)  37.3 us
    all_to_all x1, blocking collectives, all_sum(): lax.all_to_all(jnp.broadcast_to(owned[None], (devices, chunk, width)), ('...  26.6 us
    pallas_call x2, Pallas kernels, tile_sums(): pl.pallas_call(functools.partial(tile_kernel, transpose=transpose), out_s...  19.3 us
    all_to_all x1, starting transfers between devices, body(): lax.all_to_all(outgoing_rows, 'col', split_axis=0, concat_axis=0, tiled=T...  10.4 us
  transfers between devices with their start and end apart: 4, of which 3 were waited for; matrix products, arithmetic and copies ran while one was open for 2% of the time, Pallas kernels for 0%

profile of v6, /device:TPU:1, one launch (start us, length us, event | category | flops | bytes accessed | tf_op | source)
XLA Modules:
  0.0 482.1 jit_solution(8833320335564823272)
XLA Ops:
  7.2 0.0 copy-start
  7.2 0.0 all-gather.2.cloned.1.call-start
  7.2 0.7 all-gather.2.cloned.1.call-update
  8.6 0.7 maximum_add_fusion
  9.3 0.1 copy.20
  9.3 0.1 reshape.131
  9.4 0.7 compare_select_fusion.2
  10.1 1.3 gather_fusion
  11.4 37.3 %all-gather.2.cloned.1.call-done = bf16[8192,256]{1,0:T(8,128)(2,1)} async-done(((bf16[1024,256]{1,0:T(8,128)(2,1)}), bf16[8192,256]{1,0:T(8,128)(2,1)}) %all-gather.2.cloned.1.call-update) | async-done | bytes 4194320 | tf_op jit(solution)/shard_map/all_gather | solution.py:98
  48.6 0.0 copy-done
  48.7 5.5 %convolution_convert_fusion.1 = bf16[8192,256]{1,0:T(8,128)(2,1)} fusion(bf16[8192,256]{1,0:T(8,128)(2,1)} %all-gather.2.cloned.1.call-done, bf16[256,256]{1,0:T(8,128)(2,1)S(1)} %copy-done), kind=kOutput, calls=%fused_computation.4 | convolution fusion | flops 1075838976 | bytes 8519680 | tf_op jit(solution)/shard_map/dot_general | solution.py:99
  54.1 10.1 %shard_map.129 = bf16[96,128,256]{2,1,0:T(8,128)(2,1)} custom-call(s32[48]{0:T(128)} %gather_fusion, s32[48]{0:T(128)} %take_ref.1, s32[1]{0:T(128)S(6)} %copy.28.count_ref, bf16[48,128,128]{2,1,0:T(8,128)(2,1)} %adj_ref.3, bf16[64,128,256]{2,1,0:T(8,128)(2,1)} %bitcast.31), custom_call_target="tpu_custom_call" | custom-call | flops 402653184 | bytes 12058624 | tf_op jit(solution)/shard_map/pallas_call | solution.py:44
  64.2 0.0 copy-start.3
  64.2 10.4 %all-to-all-start = ((bf16[32,3,128,256]{3,2,1,0:T(8,128)(2,1)}), bf16[32,3,128,256]{3,2,1,0:T(8,128)(2,1)}, u32[]{:S(2)}, u32[]{:S(2)}) async-start(bf16[32,3,128,256]{3,2,1,0:T(8,128)(2,1)} %bitcast.28), calls=%async_computation | async-start | bytes 12582912 | tf_op jit(solution)/shard_map/all_to_all | solution.py:119
  74.6 0.0 copy-done.3
  74.6 0.1 copy.19
  74.7 0.1 copy.22
  74.8 0.1 reshape.137
  74.9 0.1 eq.28
  75.0 138.0 %all-to-all-done = bf16[32,3,128,256]{3,2,1,0:T(8,128)(2,1)} async-done(((bf16[32,3,128,256]{3,2,1,0:T(8,128)(2,1)}), bf16[32,3,128,256]{3,2,1,0:T(8,128)(2,1)}, u32[]{:S(2)}, u32[]{:S(2)}) %all-to-all-start) | async-done | bytes 6291488 | tf_op jit(solution)/shard_map/all_to_all | solution.py:119
  213.0 6.9 %copy.26 = bf16[12,8,128,256]{3,1,2,0:T(8,128)(2,1)S(1)} copy(bf16[12,8,128,256]{3,2,1,0:T(8,128)(2,1)} %bitcast.12) | data formatting | bytes 12582912
  220.0 0.0 copy-start.2
  220.0 0.0 copy-start.5
  220.0 0.9 fusion.4
  220.9 0.2 reshape.135
  221.1 0.0 copy-done.2
  221.1 0.0 copy-done.5
  221.1 1.3 fusion.8
  222.4 6.0 %gather_fusion.1 = bf16[96,128,256]{2,1,0:T(8,128)(2,1)} fusion(bf16[8,128,256]{2,1,0:T(8,128)(2,1)S(1)} %bitcast.27, s32[1024]{0:T(1024)S(1)} %pad_clamp_fusion.1), kind=kCustom, calls=%fused_computation.1 | custom fusion | bytes 12583296 | tf_op jit(solution)/shard_map/gather | solution.py:133
  228.4 0.0 copy-start.4
  228.4 9.6 %all-to-all-start.1 = ((bf16[32,3,128,256]{3,2,1,0:T(8,128)(2,1)}), bf16[32,3,128,256]{3,2,1,0:T(8,128)(2,1)}, u32[]{:S(2)}, u32[]{:S(2)}) async-start(bf16[32,3,128,256]{3,2,1,0:T(8,128)(2,1)} %bitcast.29), calls=%async_computation.1 | async-start | bytes 12582912 | tf_op jit(solution)/shard_map/all_to_all | solution.py:136
  238.0 0.2 reduce-scatter.2.cloned.1.call-start
  238.2 0.0 copy-done.4
  238.2 0.1 copy.21
  238.3 0.1 ge.11
  238.4 138.7 %all-to-all-done.1 = bf16[32,3,128,256]{3,2,1,0:T(8,128)(2,1)} async-done(((bf16[32,3,128,256]{3,2,1,0:T(8,128)(2,1)}), bf16[32,3,128,256]{3,2,1,0:T(8,128)(2,1)}, u32[]{:S(2)}, u32[]{:S(2)}) %all-to-all-start.1) | async-done | bytes 6291488 | tf_op jit(solution)/shard_map/all_to_all | solution.py:136
  377.1 9.2 %shard_map.130 = bf16[24,128,256]{2,1,0:T(8,128)(2,1)} custom-call(s32[48]{0:T(128)} %take_ref.1, s32[48]{0:T(128)} %put_ref.3, s32[1]{0:T(128)S(6)} %copy.28.count_ref, bf16[48,128,128]{2,1,0:T(8,128)(2,1)} %adj_ref.3, bf16[96,128,256]{2,1,0:T(8,128)(2,1)} %bitcast.5.operand_ref), custom_call_target="tpu_custom_call" | custom-call | flops 402653184 | bytes 9437184 | tf_op jit(solution)/shard_map/pallas_call | solution.py:44
  386.3 2.3 copy.27
  388.6 3.2 convolution_convert_fusion
  391.8 0.0 copy-start.1
  391.8 0.0 reduce-scatter.2.cloned.1.call-update
  391.8 0.1 reshape.142
  391.9 2.9 gather_fusion.2
  394.8 0.0 copy-done.1
  394.8 0.6 convolution_bitcast_fusion
  395.5 0.3 reshape.143
  395.8 48.1 %all_to_all.20 = f32[256,2,256]{2,1,0:T(2,128)S(1)} all-to-all(f32[256,2,256]{2,1,0:T(2,128)S(1)} %reshape.143), channel_id=1, replica_groups=mesh['row'=8,'col'=32] {'row','col'}, dimensions={0} | all-to-all | bytes 1048576 | tf_op jit(solution)/shard_map/all_to_all | solution.py:67
  443.9 0.3 reduce_sum.19
  444.1 0.1 broadcast_in_dim.8
  444.3 26.6 %all_to_all.21 = f32[256,2,256]{2,1,0:T(2,128)S(1)} all-to-all(f32[256,2,256]{2,1,0:T(2,128)S(1)} %broadcast_in_dim.8), channel_id=1, replica_groups=mesh['row'=8,'col'=32] {'row','col'}, dimensions={0} | all-to-all | bytes 1048576 | tf_op jit(solution)/shard_map/all_to_all | solution.py:71
  470.9 0.1 slice_multiply_fusion
  471.0 0.9 mul.46
  471.9 0.4 reshape.144
  472.2 0.6 slice_multiply_fusion.1
  472.8 0.0 reduce-scatter.2.cloned.1.call-done
  472.8 1.3 convert_element_type.32
  474.1 1.1 convolution_convert_fusion.2
  (9 shorter events, 0.1 us)
Async XLA Ops:
  7.2 41.5 %copy-start = (bf16[256,256]{1,0:T(8,128)(2,1)S(1)}, bf16[256,256]{1,0:T(8,128)(2,1)}, u32[]{:S(2)}) copy-start(bf16[256,256]{1,0:T(8,128)(2,1)} %param.11) | copy-start | bytes 393220
  7.2 41.5 %all-gather.2.cloned.1.call-start = ((), (), s32[]{:S(2)}) async-start(), calls=%async_computation.5 | async-start | bytes 4718592 | tf_op jit(solution)/shard_map/all_gather | solution.py:98
  64.2 10.4 %copy-start.3 = (s32[32,3]{0,1:T(4,128)S(1)}, s32[32,3]{0,1:T(4,128)}, u32[]{:S(2)}) copy-start(s32[32,3]{0,1:T(4,128)} %param.18) | copy-start | bytes 1156
  64.2 148.8 %all-to-all-start = ((bf16[32,3,128,256]{3,2,1,0:T(8,128)(2,1)}), bf16[32,3,128,256]{3,2,1,0:T(8,128)(2,1)}, u32[]{:S(2)}, u32[]{:S(2)}) async-start(bf16[32,3,128,256]{3,2,1,0:T(8,128)(2,1)} %bitcast.28), calls=%async_computation | async-start | bytes 12582912 | tf_op jit(solution)/shard_map/all_to_all | solution.py:119
  220.0 1.1 copy-start.2
  220.0 1.1 copy-start.5
  228.4 9.8 %copy-start.4 = (s32[8,3]{0,1:T(4,128)S(1)}, s32[8,3]{0,1:T(4,128)}, u32[]{:S(2)}) copy-start(s32[8,3]{0,1:T(4,128)} %param.17) | copy-start | bytes 292
  228.4 148.8 %all-to-all-start.1 = ((bf16[32,3,128,256]{3,2,1,0:T(8,128)(2,1)}), bf16[32,3,128,256]{3,2,1,0:T(8,128)(2,1)}, u32[]{:S(2)}, u32[]{:S(2)}) async-start(bf16[32,3,128,256]{3,2,1,0:T(8,128)(2,1)} %bitcast.29), calls=%async_computation.1 | async-start | bytes 12582912 | tf_op jit(solution)/shard_map/all_to_all | solution.py:136
  238.0 234.8 %reduce-scatter.2.cloned.1.call-start = ((), (), s32[]{:S(2)}) async-start(), calls=%async_computation.6 | async-start | bytes 4718592 | tf_op jit(solution)/shard_map/reduce_scatter | solution.py:159
  391.8 3.1 copy-start.1
Sparse Core Ops, SparseCore 0:
  9.8 38.7 all-gather.1
  391.9 57.2 reduce-scatter.1

commit v7 on v6

--- a/solution.py
+++ b/solution.py
@@ -56,6 +56,36 @@
         adj_tiles,
         operand,
     )
+
+
+def slot_add_kernel(put_ref, operand_ref, out_ref):
+    out_ref[...] = jnp.zeros_like(out_ref)
+
+    def step(s, carry):
+        block = put_ref[s]
+        out_ref[block] = out_ref[block] + operand_ref[s].astype(jnp.float32)
+        return carry
+
+    lax.fori_loop(0, operand_ref.shape[0], step, 0)
+
+
+def slot_add(operand, put_block, block_total):
+    tile_side, width = operand.shape[1:]
+    smem = pl.BlockSpec(memory_space=pltpu.SMEM)
+    vmem = pl.BlockSpec(memory_space=pltpu.VMEM)
+    summed = pl.pallas_call(
+        slot_add_kernel,
+        out_shape=jax.ShapeDtypeStruct((block_total + 1, tile_side, width), jnp.float32),
+        in_specs=[smem, vmem],
+        out_specs=vmem,
+        compiler_params=pltpu.CompilerParams(vmem_limit_bytes=32 * 1024 * 1024),
+        cost_estimate=pl.CostEstimate(
+            flops=operand.size,
+            bytes_accessed=operand.size * 2 + (block_total + 1) * tile_side * width * 4,
+            transcendentals=0,
+        ),
+    )(put_block.astype(jnp.int32), operand)
+    return summed[:block_total]
 
 
 def all_sum(weight_term, bias_term):
@@ -117,13 +147,11 @@
         col_devices, deliver_cap, tile_side, feat_width
     )
     incoming = lax.all_to_all(outgoing_rows, "col", split_axis=0, concat_axis=0, tiled=True)
-    deliver_hot = (
-        deliver_list.reshape(-1)[None, :] == jnp.arange(own_blocks, dtype=jnp.int32)[:, None]
-    ).astype(jnp.bfloat16)
-    aggregated = jnp.dot(
-        deliver_hot,
-        incoming.reshape(col_devices * deliver_cap, block_cells),
-        preferred_element_type=jnp.float32,
+    deliver_flat = deliver_list.reshape(-1)
+    aggregated = slot_add(
+        incoming.reshape(col_devices * deliver_cap, tile_side, feat_width),
+        jnp.where(deliver_flat >= 0, deliver_flat, own_blocks),
+        own_blocks,
     )
     pre_act = aggregated.reshape(node_rows, feat_width) + layer_bias
     layer_out = jax.nn.silu(pre_act).astype(jnp.bfloat16)

time: 482 us -> 471 us (0.977)
  blocking collectives: 74.6 us -> 58.6 us
  Pallas kernels: 19.3 us -> 32 us
  local copies, waits for them, and re-layouts: 23.4 us -> 16.4 us
    all_to_all x1, blocking collectives: 48.1 us -> 32 us  [all_sum(): lax.all_to_all(packed.reshape(devices, chunk, width), ('row', 'col'), 0,...]
    pallas_call x2, Pallas kernels: 19.3 us -> 27.7 us  [tile_sums(): pl.pallas_call(functools.partial(tile_kernel, transpose=transpose), out_s...]
    unnamed x15 -> x14, local copies, waits for them, and re-layouts: 9.33 us -> 2.41 us
where the time goes in v7:
time: 471 us; the launch traced here: 469 us
  waiting for transfers between devices  316 us (67%)
  blocking collectives  58.6 us (12%)
  Pallas kernels  32 us (7%)
  starting transfers between devices  17.6 us (4%)
  local copies, waits for them, and re-layouts  16.4 us (3%)
  between operations  14.9 us (3%)
  matrix products  10.4 us (2%)
    all_to_all x1, waiting for transfers between devices, body(): lax.all_to_all(wanted_rows, 'col', split_axis=0, concat_axis=0, tiled=True)  139 us
    all_to_all x1, waiting for transfers between devices, body(): lax.all_to_all(outgoing_rows, 'col', split_axis=0, concat_axis=0, tiled=T...  139 us
    all_gather x1, waiting for transfers between devices, body(): column_features = lax.all_gather(features, 'row', axis=0, tiled=True)  37.3 us
    all_to_all x1, blocking collectives, all_sum(): lax.all_to_all(packed.reshape(devices, chunk, width), ('row', 'col'), 0,...  32 us
    pallas_call x2, Pallas kernels, tile_sums(): pl.pallas_call(functools.partial(tile_kernel, transpose=transpose), out_s...  27.7 us
    all_to_all x1, blocking collectives, all_sum(): lax.all_to_all(jnp.broadcast_to(owned[None], (devices, chunk, width)), ('...  26.6 us
    all_to_all x1, starting transfers between devices, body(): lax.all_to_all(wanted_rows, 'col', split_axis=0, concat_axis=0, tiled=True)  10.2 us
  transfers between devices with their start and end apart: 4, of which 3 were waited for; matrix products, arithmetic and copies ran while one was open for 2% of the time, Pallas kernels for 0%

profile of v7, /device:TPU:1, one launch (start us, length us, event | category | flops | bytes accessed | tf_op | source)
XLA Modules:
  0.0 469.1 jit_solution(11167584167114827829)
XLA Ops:
  7.2 0.0 copy-start
  7.2 0.0 all-gather.2.cloned.1.call-start
  7.2 0.7 all-gather.2.cloned.1.call-update
  8.6 0.7 maximum_add_fusion
  9.3 0.1 copy.20
  9.3 0.1 reshape.134
  9.4 0.7 compare_select_fusion.2
  10.1 1.3 gather_fusion
  11.4 37.3 %all-gather.2.cloned.1.call-done = bf16[8192,256]{1,0:T(8,128)(2,1)} async-done(((bf16[1024,256]{1,0:T(8,128)(2,1)}), bf16[8192,256]{1,0:T(8,128)(2,1)}) %all-gather.2.cloned.1.call-update) | async-done | bytes 4194320 | tf_op jit(solution)/shard_map/all_gather | solution.py:128
  48.6 0.0 copy-done
  48.7 5.5 %convolution_convert_fusion.1 = bf16[8192,256]{1,0:T(8,128)(2,1)} fusion(bf16[8192,256]{1,0:T(8,128)(2,1)} %all-gather.2.cloned.1.call-done, bf16[256,256]{1,0:T(8,128)(2,1)S(1)} %copy-done), kind=kOutput, calls=%fused_computation.4 | convolution fusion | flops 1075838976 | bytes 8519680 | tf_op jit(solution)/shard_map/dot_general | solution.py:129
  54.1 13.7 %shard_map.129 = bf16[96,128,256]{2,1,0:T(8,128)(2,1)} custom-call(s32[48]{0:T(128)} %gather_fusion, s32[48]{0:T(128)} %take_ref.1, s32[1]{0:T(128)S(6)} %copy.27.count_ref, bf16[48,128,128]{2,1,0:T(8,128)(2,1)} %adj_ref.3, bf16[64,128,256]{2,1,0:T(8,128)(2,1)} %bitcast.34), custom_call_target="tpu_custom_call" | custom-call | flops 402653184 | bytes 12058624 | tf_op jit(solution)/shard_map/pallas_call | solution.py:44
  67.9 0.0 copy-start.3
  67.9 7.4 %all-to-all-start = ((bf16[32,3,128,256]{3,2,1,0:T(8,128)(2,1)}), bf16[32,3,128,256]{3,2,1,0:T(8,128)(2,1)}, u32[]{:S(2)}, u32[]{:S(2)}) async-start(bf16[32,3,128,256]{3,2,1,0:T(8,128)(2,1)} %bitcast.32), calls=%async_computation | async-start | bytes 12582912 | tf_op jit(solution)/shard_map/all_to_all | solution.py:149
  75.2 0.0 copy-done.3
  75.3 0.1 copy.19
  75.3 0.1 copy.22
  75.4 0.1 reshape.140
  75.5 0.1 reshape.133
  75.7 138.8 %all-to-all-done = bf16[32,3,128,256]{3,2,1,0:T(8,128)(2,1)} async-done(((bf16[32,3,128,256]{3,2,1,0:T(8,128)(2,1)}), bf16[32,3,128,256]{3,2,1,0:T(8,128)(2,1)}, u32[]{:S(2)}, u32[]{:S(2)}) %all-to-all-start) | async-done | bytes 6291488 | tf_op jit(solution)/shard_map/all_to_all | solution.py:149
  214.5 0.0 copy-start.2
  214.5 0.0 copy-start.5
  214.5 4.3 shard_map.130
  218.8 0.1 slice.19
  218.9 0.0 copy-done.2
  218.9 0.0 copy-done.5
  218.9 1.3 fusion.6
  220.3 5.9 %gather_fusion.1 = bf16[96,128,256]{2,1,0:T(8,128)(2,1)} fusion(bf16[8,128,256]{2,1,0:T(8,128)(2,1)S(1)} %bitcast.31, s32[1024]{0:T(1024)S(1)} %pad_clamp_fusion.1), kind=kCustom, calls=%fused_computation.1 | custom fusion | bytes 12583296 | tf_op jit(solution)/shard_map/gather | solution.py:161
  226.2 0.0 copy-start.4
  226.2 10.2 %all-to-all-start.1 = ((bf16[32,3,128,256]{3,2,1,0:T(8,128)(2,1)}), bf16[32,3,128,256]{3,2,1,0:T(8,128)(2,1)}, u32[]{:S(2)}, u32[]{:S(2)}) async-start(bf16[32,3,128,256]{3,2,1,0:T(8,128)(2,1)} %bitcast.33), calls=%async_computation.1 | async-start | bytes 12582912 | tf_op jit(solution)/shard_map/all_to_all | solution.py:164
  236.4 0.0 reduce-scatter.2.cloned.1.call-start
  236.4 0.0 copy-done.4
  236.4 0.1 copy.21
  236.5 0.1 ge.15
  236.6 138.8 %all-to-all-done.1 = bf16[32,3,128,256]{3,2,1,0:T(8,128)(2,1)} async-done(((bf16[32,3,128,256]{3,2,1,0:T(8,128)(2,1)}), bf16[32,3,128,256]{3,2,1,0:T(8,128)(2,1)}, u32[]{:S(2)}, u32[]{:S(2)}) %all-to-all-start.1) | async-done | bytes 6291488 | tf_op jit(solution)/shard_map/all_to_all | solution.py:164
  375.5 14.0 %shard_map.131 = bf16[24,128,256]{2,1,0:T(8,128)(2,1)} custom-call(s32[48]{0:T(128)} %take_ref.1, s32[48]{0:T(128)} %put_ref.3, s32[1]{0:T(128)S(6)} %copy.27.count_ref, bf16[48,128,128]{2,1,0:T(8,128)(2,1)} %adj_ref.3, bf16[96,128,256]{2,1,0:T(8,128)(2,1)} %bitcast.7.operand_ref), custom_call_target="tpu_custom_call" | custom-call | flops 402653184 | bytes 9437184 | tf_op jit(solution)/shard_map/pallas_call | solution.py:44
  389.4 2.3 copy.26
  391.7 3.2 convolution_convert_fusion
  394.9 0.0 copy-start.1
  394.9 0.0 reduce-scatter.2.cloned.1.call-update
  394.9 0.1 reshape.145
  395.0 2.9 gather_fusion.2
  398.0 0.0 copy-done.1
  398.0 0.6 convolution_bitcast_fusion
  398.6 0.3 reshape.146
  399.0 32.0 %all_to_all.20 = f32[256,2,256]{2,1,0:T(2,128)S(1)} all-to-all(f32[256,2,256]{2,1,0:T(2,128)S(1)} %reshape.146), channel_id=1, replica_groups=mesh['row'=8,'col'=32] {'row','col'}, dimensions={0} | all-to-all | bytes 1048576 | tf_op jit(solution)/shard_map/all_to_all | solution.py:97
  430.9 0.3 reduce_sum.19
  431.2 0.1 broadcast_in_dim.28
  431.4 26.6 %all_to_all.21 = f32[256,2,256]{2,1,0:T(2,128)S(1)} all-to-all(f32[256,2,256]{2,1,0:T(2,128)S(1)} %broadcast_in_dim.28), channel_id=1, replica_groups=mesh['row'=8,'col'=32] {'row','col'}, dimensions={0} | all-to-all | bytes 1048576 | tf_op jit(solution)/shard_map/all_to_all | solution.py:101
  457.9 0.1 slice_multiply_fusion
  458.1 0.9 mul.46
  458.9 0.4 reshape.147
  459.3 0.6 slice_multiply_fusion.1
  459.9 0.0 reduce-scatter.2.cloned.1.call-done
  459.9 1.3 convert_element_type.31
  461.2 1.1 convolution_convert_fusion.2
  (10 shorter events, 0.1 us)
Async XLA Ops:
  7.2 41.5 %copy-start = (bf16[256,256]{1,0:T(8,128)(2,1)S(1)}, bf16[256,256]{1,0:T(8,128)(2,1)}, u32[]{:S(2)}) copy-start(bf16[256,256]{1,0:T(8,128)(2,1)} %param.11) | copy-start | bytes 393220
  7.2 41.5 %all-gather.2.cloned.1.call-start = ((), (), s32[]{:S(2)}) async-start(), calls=%async_computation.5 | async-start | bytes 4718592 | tf_op jit(solution)/shard_map/all_gather | solution.py:128
  67.9 7.4 %copy-start.3 = (s32[32,3]{0,1:T(4,128)S(1)}, s32[32,3]{0,1:T(4,128)}, u32[]{:S(2)}) copy-start(s32[32,3]{0,1:T(4,128)} %param.18) | copy-start | bytes 1156
  67.9 146.7 %all-to-all-start = ((bf16[32,3,128,256]{3,2,1,0:T(8,128)(2,1)}), bf16[32,3,128,256]{3,2,1,0:T(8,128)(2,1)}, u32[]{:S(2)}, u32[]{:S(2)}) async-start(bf16[32,3,128,256]{3,2,1,0:T(8,128)(2,1)} %bitcast.32), calls=%async_computation | async-start | bytes 12582912 | tf_op jit(solution)/shard_map/all_to_all | solution.py:149
  214.5 4.4 copy-start.2
  214.5 4.4 copy-start.5
  226.2 10.2 %copy-start.4 = (s32[8,3]{0,1:T(4,128)S(1)}, s32[8,3]{0,1:T(4,128)}, u32[]{:S(2)}) copy-start(s32[8,3]{0,1:T(4,128)} %param.17) | copy-start | bytes 292
  226.2 149.3 %all-to-all-start.1 = ((bf16[32,3,128,256]{3,2,1,0:T(8,128)(2,1)}), bf16[32,3,128,256]{3,2,1,0:T(8,128)(2,1)}, u32[]{:S(2)}, u32[]{:S(2)}) async-start(bf16[32,3,128,256]{3,2,1,0:T(8,128)(2,1)} %bitcast.33), calls=%async_computation.1 | async-start | bytes 12582912 | tf_op jit(solution)/shard_map/all_to_all | solution.py:164
  236.4 223.5 %reduce-scatter.2.cloned.1.call-start = ((), (), s32[]{:S(2)}) async-start(), calls=%async_computation.6 | async-start | bytes 4718592 | tf_op jit(solution)/shard_map/reduce_scatter | solution.py:187
  394.9 3.1 copy-start.1
Sparse Core Ops, SparseCore 0:
  9.8 38.7 all-gather.1
  395.1 41.1 reduce-scatter.1

commit v8 on v7

--- a/solution.py
+++ b/solution.py
@@ -86,6 +86,32 @@
         ),
     )(put_block.astype(jnp.int32), operand)
     return summed[:block_total]
+
+
+def slot_take_kernel(take_ref, source_ref, out_ref):
+    def step(s, carry):
+        out_ref[s] = source_ref[take_ref[s]]
+        return carry
+
+    lax.fori_loop(0, out_ref.shape[0], step, 0)
+
+
+def slot_take(source, take_block):
+    slots = take_block.shape[0]
+    smem = pl.BlockSpec(memory_space=pltpu.SMEM)
+    vmem = pl.BlockSpec(memory_space=pltpu.VMEM)
+    return pl.pallas_call(
+        slot_take_kernel,
+        out_shape=jax.ShapeDtypeStruct((slots,) + source.shape[1:], source.dtype),
+        in_specs=[smem, vmem],
+        out_specs=vmem,
+        compiler_params=pltpu.CompilerParams(vmem_limit_bytes=32 * 1024 * 1024),
+        cost_estimate=pl.CostEstimate(
+            flops=0,
+            bytes_accessed=(source.size + slots * source[0].size) * source.dtype.itemsize,
+            transcendentals=0,
+        ),
+    )(take_block.astype(jnp.int32), source)
 
 
 def all_sum(weight_term, bias_term):
@@ -158,7 +184,7 @@
     slopes = cotangent.astype(jnp.float32) * silu_grad(pre_act)
     bias_term = jnp.sum(slopes, axis=0)
     slope_blocks = slopes.astype(jnp.bfloat16).reshape(own_blocks, tile_side, feat_width)
-    wanted_rows = slope_blocks[jnp.maximum(deliver_list, 0).reshape(-1)].reshape(
+    wanted_rows = slot_take(slope_blocks, jnp.maximum(deliver_flat, 0)).reshape(
         col_devices, deliver_cap, tile_side, feat_width
     )
     row_values = lax.all_to_all(

time: 471 us -> 477 us (1.013)
  blocking collectives: 58.6 us -> 73.1 us
  Pallas kernels: 32 us -> 20.7 us
    all_to_all x1, blocking collectives: 32 us -> 46.5 us  [all_sum(): lax.all_to_all(packed.reshape(devices, chunk, width), ('row', 'col'), 0,...]
    pallas_call x2, Pallas kernels: 27.7 us -> 15.1 us  [tile_sums(): pl.pallas_call(functools.partial(tile_kernel, transpose=transpose), out_s...]
    gather x1 -> x0, local copies, waits for them, and re-layouts: 5.94 us -> none  [body(): slope_blocks[jnp.maximum(deliver_list, 0).reshape(-1)]]
    all_to_all x1, starting transfers between devices: 7.38 us -> 13.1 us  [body(): lax.all_to_all(outgoing_rows, 'col', split_axis=0, concat_axis=0, tiled=T...]
where the time goes in v8:
time: 477 us; the launch traced here: 475 us
  waiting for transfers between devices  317 us (66%)
  blocking collectives  73.1 us (15%)
  starting transfers between devices  21.2 us (4%)
  Pallas kernels  20.7 us (4%)
  between operations  14.9 us (3%)
  local copies, waits for them, and re-layouts  13.8 us (3%)
  matrix products  10.4 us (2%)
    all_to_all x1, waiting for transfers between devices, body(): lax.all_to_all(outgoing_rows, 'col', split_axis=0, concat_axis=0, tiled=T...  140 us
    all_to_all x1, waiting for transfers between devices, body(): lax.all_to_all(wanted_rows, 'col', split_axis=0, concat_axis=0, tiled=True)  139 us
    all_to_all x1, blocking collectives, all_sum(): lax.all_to_all(packed.reshape(devices, chunk, width), ('row', 'col'), 0,...  46.5 us
    all_gather x1, waiting for transfers between devices, body(): column_features = lax.all_gather(features, 'row', axis=0, tiled=True)  37.3 us
    all_to_all x1, blocking collectives, all_sum(): lax.all_to_all(jnp.broadcast_to(owned[None], (devices, chunk, width)), ('...  26.6 us
    pallas_call x2, Pallas kernels, tile_sums(): pl.pallas_call(functools.partial(tile_kernel, transpose=transpose), out_s...  15.1 us
    all_to_all x1, starting transfers between devices, body(): lax.all_to_all(outgoing_rows, 'col', split_axis=0, concat_axis=0, tiled=T...  13.1 us
  transfers between devices with their start and end apart: 4, of which 3 were waited for; matrix products, arithmetic and copies ran while one was open for 2% of the time, Pallas kernels for 0%

profile of v8, /device:TPU:1, one launch (start us, length us, event | category | flops | bytes accessed | tf_op | source)
XLA Modules:
  0.0 474.7 jit_solution(5400469877862255735)
XLA Ops:
  7.2 0.0 copy-start
  7.2 0.0 all-gather.2.cloned.1.call-start
  7.2 0.7 all-gather.2.cloned.1.call-update
  8.6 0.7 maximum_add_fusion
  9.3 0.1 copy.19
  9.3 0.1 reshape.103
  9.4 0.7 compare_select_fusion.1
  10.1 1.3 gather_fusion
  11.4 37.3 %all-gather.2.cloned.1.call-done = bf16[8192,256]{1,0:T(8,128)(2,1)} async-done(((bf16[1024,256]{1,0:T(8,128)(2,1)}), bf16[8192,256]{1,0:T(8,128)(2,1)}) %all-gather.2.cloned.1.call-update) | async-done | bytes 4194320 | tf_op jit(solution)/shard_map/all_gather | solution.py:154
  48.6 0.0 copy-done
  48.7 5.5 %convolution_convert_fusion.1 = bf16[8192,256]{1,0:T(8,128)(2,1)} fusion(bf16[8192,256]{1,0:T(8,128)(2,1)} %all-gather.2.cloned.1.call-done, bf16[256,256]{1,0:T(8,128)(2,1)S(1)} %copy-done), kind=kOutput, calls=%fused_computation.3 | convolution fusion | flops 1075838976 | bytes 8519680 | tf_op jit(solution)/shard_map/dot_general | solution.py:155
  54.1 8.3 %shard_map.129 = bf16[96,128,256]{2,1,0:T(8,128)(2,1)} custom-call(s32[48]{0:T(128)} %gather_fusion, s32[48]{0:T(128)} %take_ref.1, s32[1]{0:T(128)S(6)} %copy.25.count_ref, bf16[48,128,128]{2,1,0:T(8,128)(2,1)} %adj_ref.3, bf16[64,128,256]{2,1,0:T(8,128)(2,1)} %bitcast.32), custom_call_target="tpu_custom_call" | custom-call | flops 402653184 | bytes 12058624 | tf_op jit(solution)/shard_map/pallas_call | solution.py:44
  62.4 0.0 copy-start.5
  62.4 13.1 %all-to-all-start = ((bf16[32,3,128,256]{3,2,1,0:T(8,128)(2,1)}), bf16[32,3,128,256]{3,2,1,0:T(8,128)(2,1)}, u32[]{:S(2)}, u32[]{:S(2)}) async-start(bf16[32,3,128,256]{3,2,1,0:T(8,128)(2,1)} %bitcast.31), calls=%async_computation | async-start | bytes 12582912 | tf_op jit(solution)/shard_map/all_to_all | solution.py:175
  75.5 0.0 copy-done.5
  75.5 0.1 copy.18
  75.6 0.1 reshape.102
  75.7 140.2 %all-to-all-done = bf16[32,3,128,256]{3,2,1,0:T(8,128)(2,1)} async-done(((bf16[32,3,128,256]{3,2,1,0:T(8,128)(2,1)}), bf16[32,3,128,256]{3,2,1,0:T(8,128)(2,1)}, u32[]{:S(2)}, u32[]{:S(2)}) %all-to-all-start) | async-done | bytes 6291488 | tf_op jit(solution)/shard_map/all_to_all | solution.py:175
  215.9 4.2 shard_map.130
  220.1 0.0 copy-start.3
  220.2 0.0 copy-start.6
  220.2 0.1 slice.17
  220.3 0.9 copy-done.3
  221.2 0.0 copy-done.6
  221.2 1.3 fusion.5
  222.5 1.4 shard_map.131
  223.9 0.0 copy-start.1
  223.9 2.6 copy-done.1
  226.6 0.0 copy-start.4
  226.6 8.0 %all-to-all-start.1 = ((bf16[32,3,128,256]{3,2,1,0:T(8,128)(2,1)}), bf16[32,3,128,256]{3,2,1,0:T(8,128)(2,1)}, u32[]{:S(2)}, u32[]{:S(2)}) async-start(bf16[32,3,128,256]{3,2,1,0:T(8,128)(2,1)} %bitcast.29), calls=%async_computation.1 | async-start | bytes 12582912 | tf_op jit(solution)/shard_map/all_to_all | solution.py:190
  234.6 0.0 reduce-scatter.2.cloned.1.call-start
  234.6 0.0 copy-done.4
  234.6 0.1 copy.20
  234.7 0.1 ge.15
  234.8 138.9 %all-to-all-done.1 = bf16[32,3,128,256]{3,2,1,0:T(8,128)(2,1)} async-done(((bf16[32,3,128,256]{3,2,1,0:T(8,128)(2,1)}), bf16[32,3,128,256]{3,2,1,0:T(8,128)(2,1)}, u32[]{:S(2)}, u32[]{:S(2)}) %all-to-all-start.1) | async-done | bytes 6291488 | tf_op jit(solution)/shard_map/all_to_all | solution.py:190
  373.7 6.8 %shard_map.132 = bf16[24,128,256]{2,1,0:T(8,128)(2,1)} custom-call(s32[48]{0:T(128)} %take_ref.1, s32[48]{0:T(128)} %put_ref.3, s32[1]{0:T(128)S(6)} %copy.25.count_ref, bf16[48,128,128]{2,1,0:T(8,128)(2,1)} %adj_ref.3, bf16[96,128,256]{2,1,0:T(8,128)(2,1)} %bitcast.6.operand_ref), custom_call_target="tpu_custom_call" | custom-call | flops 402653184 | bytes 9437184 | tf_op jit(solution)/shard_map/pallas_call | solution.py:44
  380.5 2.3 copy.24
  382.8 3.2 convolution_convert_fusion
  386.0 0.0 reduce-scatter.2.cloned.1.call-update
  386.0 0.1 reshape.113
  386.1 0.0 copy-start.2
  386.1 3.0 gather_fusion.1
  389.1 0.0 copy-done.2
  389.1 0.6 convolution_bitcast_fusion
  389.7 0.3 reshape.114
  390.0 46.5 %all_to_all.20 = f32[256,2,256]{2,1,0:T(2,128)S(1)} all-to-all(f32[256,2,256]{2,1,0:T(2,128)S(1)} %reshape.114), channel_id=1, replica_groups=mesh['row'=8,'col'=32] {'row','col'}, dimensions={0} | all-to-all | bytes 1048576 | tf_op jit(solution)/shard_map/all_to_all | solution.py:123
  436.5 0.3 reduce_sum.19
  436.8 0.1 broadcast_in_dim.24
  437.0 26.6 %all_to_all.21 = f32[256,2,256]{2,1,0:T(2,128)S(1)} all-to-all(f32[256,2,256]{2,1,0:T(2,128)S(1)} %broadcast_in_dim.24), channel_id=1, replica_groups=mesh['row'=8,'col'=32] {'row','col'}, dimensions={0} | all-to-all | bytes 1048576 | tf_op jit(solution)/shard_map/all_to_all | solution.py:127
  463.6 0.1 slice_multiply_fusion
  463.7 0.9 mul.46
  464.6 0.4 reshape.115
  464.9 0.6 slice_multiply_fusion.1
  465.5 0.0 reduce-scatter.2.cloned.1.call-done
  465.5 1.3 convert_element_type.31
  466.8 1.1 convolution_convert_fusion.2
  (7 shorter events, 0.1 us)
Async XLA Ops:
  7.2 41.5 %copy-start = (bf16[256,256]{1,0:T(8,128)(2,1)S(1)}, bf16[256,256]{1,0:T(8,128)(2,1)}, u32[]{:S(2)}) copy-start(bf16[256,256]{1,0:T(8,128)(2,1)} %param.11) | copy-start | bytes 393220
  7.2 41.5 %all-gather.2.cloned.1.call-start = ((), (), s32[]{:S(2)}) async-start(), calls=%async_computation.5 | async-start | bytes 4718592 | tf_op jit(solution)/shard_map/all_gather | solution.py:154
  62.4 13.1 %copy-start.5 = (s32[32,3]{0,1:T(4,128)S(1)}, s32[32,3]{0,1:T(4,128)}, u32[]{:S(2)}) copy-start(s32[32,3]{0,1:T(4,128)} %param.18) | copy-start | bytes 1156
  62.4 153.5 %all-to-all-start = ((bf16[32,3,128,256]{3,2,1,0:T(8,128)(2,1)}), bf16[32,3,128,256]{3,2,1,0:T(8,128)(2,1)}, u32[]{:S(2)}, u32[]{:S(2)}) async-start(bf16[32,3,128,256]{3,2,1,0:T(8,128)(2,1)} %bitcast.31), calls=%async_computation | async-start | bytes 12582912 | tf_op jit(solution)/shard_map/all_to_all | solution.py:175
  220.1 1.0 copy-start.3
  220.2 1.0 copy-start.6
  223.9 2.7 copy-start.1
  226.6 8.0 %copy-start.4 = (s32[8,3]{0,1:T(4,128)S(1)}, s32[8,3]{0,1:T(4,128)}, u32[]{:S(2)}) copy-start(s32[8,3]{0,1:T(4,128)} %param.17) | copy-start | bytes 292
  226.6 147.1 %all-to-all-start.1 = ((bf16[32,3,128,256]{3,2,1,0:T(8,128)(2,1)}), bf16[32,3,128,256]{3,2,1,0:T(8,128)(2,1)}, u32[]{:S(2)}, u32[]{:S(2)}) async-start(bf16[32,3,128,256]{3,2,1,0:T(8,128)(2,1)} %bitcast.29), calls=%async_computation.1 | async-start | bytes 12582912 | tf_op jit(solution)/shard_map/all_to_all | solution.py:190
  234.6 230.9 %reduce-scatter.2.cloned.1.call-start = ((), (), s32[]{:S(2)}) async-start(), calls=%async_computation.6 | async-start | bytes 4718592 | tf_op jit(solution)/shard_map/reduce_scatter | solution.py:213
  386.1 3.0 copy-start.2
Sparse Core Ops, SparseCore 0:
  9.8 38.7 all-gather.1
  386.1 55.7 reduce-scatter.1

commit v9 on v8

--- a/solution.py
+++ b/solution.py
@@ -14,10 +14,12 @@
     return logistic * (1.0 + values * (1.0 - logistic))
 
 
-def tile_kernel(take_ref, put_ref, count_ref, adj_ref, operand_ref, out_ref, acc_ref, *, transpose):
-    acc_ref[...] = jnp.zeros_like(acc_ref)
-
-    def step(k, carry):
+def tile_kernel(order_ref, take_ref, put_ref, count_ref, adj_ref, operand_ref, out_ref, acc_ref, *, transpose):
+    out_ref[...] = jnp.zeros_like(out_ref)
+    count = count_ref[0]
+
+    def step(i, carry):
+        k = order_ref[i]
         tile = adj_ref[k]
         picked = operand_ref[take_ref[k]]
         if transpose:
@@ -27,31 +29,50 @@
         else:
             product = jnp.dot(tile, picked, preferred_element_type=jnp.float32)
         slot = put_ref[k]
-        acc_ref[slot] = acc_ref[slot] + product
+        previous = put_ref[order_ref[jnp.maximum(i - 1, 0)]]
+        following = put_ref[order_ref[jnp.minimum(i + 1, count - 1)]]
+        first = jnp.logical_or(i == 0, previous != slot)
+        last = jnp.logical_or(i == count - 1, following != slot)
+
+        @pl.when(first)
+        def _():
+            acc_ref[...] = product
+
+        @pl.when(jnp.logical_not(first))
+        def _():
+            acc_ref[...] = acc_ref[...] + product
+
+        @pl.when(last)
+        def _():
+            out_ref[slot] = acc_ref[...].astype(out_ref.dtype)
+
         return carry
 
-    lax.fori_loop(0, count_ref[0], step, 0)
-    out_ref[...] = acc_ref[...].astype(out_ref.dtype)
+    lax.fori_loop(0, count, step, 0)
 
 
 def tile_sums(adj_tiles, operand, take_slot, put_slot, live_count, slot_total, transpose):
-    tile_side = adj_tiles.shape[1]
+    tile_total, tile_side = adj_tiles.shape[:2]
     width = operand.shape[-1]
+    put_slot = put_slot.astype(jnp.int32)
+    live = jnp.arange(tile_total, dtype=jnp.int32) < live_count
+    order = jnp.argsort(jnp.where(live, put_slot, slot_total), stable=True).astype(jnp.int32)
     smem = pl.BlockSpec(memory_space=pltpu.SMEM)
     vmem = pl.BlockSpec(memory_space=pltpu.VMEM)
-    flops = 2 * adj_tiles.shape[0] * tile_side * tile_side * width
+    flops = 2 * tile_total * tile_side * tile_side * width
     moved = (adj_tiles.size + operand.size + slot_total * tile_side * width) * 2
     return pl.pallas_call(
         functools.partial(tile_kernel, transpose=transpose),
         out_shape=jax.ShapeDtypeStruct((slot_total, tile_side, width), jnp.bfloat16),
-        in_specs=[smem, smem, smem, vmem, vmem],
+        in_specs=[smem, smem, smem, smem, vmem, vmem],
         out_specs=vmem,
-        scratch_shapes=[pltpu.VMEM((slot_total, tile_side, width), jnp.float32)],
+        scratch_shapes=[pltpu.VMEM((tile_side, width), jnp.float32)],
         compiler_params=pltpu.CompilerParams(vmem_limit_bytes=56 * 1024 * 1024),
         cost_estimate=pl.CostEstimate(flops=flops, bytes_accessed=moved, transcendentals=0),
     )(
+        order,
         take_slot.astype(jnp.int32),
-        put_slot.astype(jnp.int32),
+        put_slot,
         jnp.reshape(live_count, (1,)).astype(jnp.int32),
         adj_tiles,
         operand,

time: 477 us -> 474 us (level)
  blocking collectives: 73.1 us -> 63.6 us
    all_to_all x1, blocking collectives: 46.5 us -> 37 us  [all_sum(): lax.all_to_all(packed.reshape(devices, chunk, width), ('row', 'col'), 0,...]
  transfers between devices with their start and end apart: 4 -> 4, of which waited for: 3 -> 3; matrix products, arithmetic and copies ran while one was open for 2% -> 3% of each run, Pallas kernels for 0% -> 0%
where the time goes in v9:
time: 474 us; the launch traced here: 471 us
  waiting for transfers between devices  314 us (66%)
  blocking collectives  63.6 us (13%)
  Pallas kernels  23.5 us (5%)
  starting transfers between devices  22.5 us (5%)
  between operations  14.9 us (3%)
  local copies, waits for them, and re-layouts  13.8 us (3%)
  matrix products  10.4 us (2%)
  other arithmetic  7.79 us (2%)
    all_to_all x1, waiting for transfers between devices, body(): lax.all_to_all(outgoing_rows, 'col', split_axis=0, concat_axis=0, tiled=T...  142 us
    all_to_all x1, waiting for transfers between devices, body(): lax.all_to_all(wanted_rows, 'col', split_axis=0, concat_axis=0, tiled=True)  136 us
    all_to_all x1, blocking collectives, all_sum(): lax.all_to_all(packed.reshape(devices, chunk, width), ('row', 'col'), 0,...  37 us
    all_gather x1, waiting for transfers between devices, body(): column_features = lax.all_gather(features, 'row', axis=0, tiled=True)  35.3 us
    all_to_all x1, blocking collectives, all_sum(): lax.all_to_all(jnp.broadcast_to(owned[None], (devices, chunk, width)), ('...  26.6 us
    pallas_call x2, Pallas kernels, tile_sums(): pl.pallas_call(functools.partial(tile_kernel, transpose=transpose), out_s...  17.8 us
    all_to_all x1, starting transfers between devices, body(): lax.all_to_all(outgoing_rows, 'col', split_axis=0, concat_axis=0, tiled=T...  12.1 us
    all_to_all x1, starting transfers between devices, body(): lax.all_to_all(wanted_rows, 'col', split_axis=0, concat_axis=0, tiled=True)  10.3 us
  transfers between devices with their start and end apart: 4, of which 3 were waited for; matrix products, arithmetic and copies ran while one was open for 3% of the time, Pallas kernels for 0%

profile of v9, /device:TPU:1, one launch (start us, length us, event | category | flops | bytes accessed | tf_op | source)
XLA Modules:
  0.0 470.8 jit_solution(14067382631920401466)
XLA Ops:
  7.2 0.0 copy-start
  7.2 0.0 all-gather.2.cloned.1.call-start
  7.2 0.7 all-gather.2.cloned.1.call-update
  8.6 0.7 maximum_add_fusion
  9.3 0.1 copy.19
  9.3 0.1 reshape.103
  9.4 0.7 compare_select_fusion.3
  10.1 2.0 sort.31
  12.2 1.3 gather_fusion
  13.4 35.3 %all-gather.2.cloned.1.call-done = bf16[8192,256]{1,0:T(8,128)(2,1)} async-done(((bf16[1024,256]{1,0:T(8,128)(2,1)}), bf16[8192,256]{1,0:T(8,128)(2,1)}) %all-gather.2.cloned.1.call-update) | async-done | bytes 4194320 | tf_op jit(solution)/shard_map/all_gather | solution.py:175
  48.7 0.0 copy-done
  48.7 5.5 %convolution_convert_fusion.1 = bf16[8192,256]{1,0:T(8,128)(2,1)} fusion(bf16[8192,256]{1,0:T(8,128)(2,1)} %all-gather.2.cloned.1.call-done, bf16[256,256]{1,0:T(8,128)(2,1)S(1)} %copy-done), kind=kOutput, calls=%fused_computation.3 | convolution fusion | flops 1075838976 | bytes 8519680 | tf_op jit(solution)/shard_map/dot_general | solution.py:176
  54.2 9.1 %shard_map.129 = bf16[96,128,256]{2,1,0:T(8,128)(2,1)} custom-call(s32[48]{0:T(128)} %get-tuple-element.6.order_ref, s32[48]{0:T(128)} %gather_fusion, s32[48]{0:T(128)} %take_ref.1, s32[1]{0:T(128)} %copy.25.count_ref, bf16[48,128,128]{2,1,0:T(8,128)(2,1)} %adj_ref.3, bf16[64,128,256]{2,1,0:T(8,128)(2,1)} %bitcast.34), custom_call_target="tpu_custom_call" | custom-call | flops 402653184 | bytes 12058624 | tf_op jit(solution)/shard_map/pallas_call | solution.py:64
  63.3 0.0 copy-start.5
  63.3 12.1 %all-to-all-start = ((bf16[32,3,128,256]{3,2,1,0:T(8,128)(2,1)}), bf16[32,3,128,256]{3,2,1,0:T(8,128)(2,1)}, u32[]{:S(2)}, u32[]{:S(2)}) async-start(bf16[32,3,128,256]{3,2,1,0:T(8,128)(2,1)} %bitcast.33), calls=%async_computation | async-start | bytes 12582912 | tf_op jit(solution)/shard_map/all_to_all | solution.py:196
  75.3 0.0 copy-done.5
  75.3 0.1 copy.18
  75.4 0.1 reshape.102
  75.6 142.2 %all-to-all-done = bf16[32,3,128,256]{3,2,1,0:T(8,128)(2,1)} async-done(((bf16[32,3,128,256]{3,2,1,0:T(8,128)(2,1)}), bf16[32,3,128,256]{3,2,1,0:T(8,128)(2,1)}, u32[]{:S(2)}, u32[]{:S(2)}) %all-to-all-start) | async-done | bytes 6291488 | tf_op jit(solution)/shard_map/all_to_all | solution.py:196
  217.8 4.2 shard_map.130
  222.0 0.0 copy-start.3
  222.0 0.0 copy-start.6
  222.0 0.1 slice.17
  222.1 0.9 copy-done.3
  223.1 0.0 copy-done.6
  223.1 1.3 fusion.5
  224.4 1.4 shard_map.131
  225.8 0.0 copy-start.1
  225.8 2.6 copy-done.1
  228.4 0.0 copy-start.4
  228.4 10.3 %all-to-all-start.1 = ((bf16[32,3,128,256]{3,2,1,0:T(8,128)(2,1)}), bf16[32,3,128,256]{3,2,1,0:T(8,128)(2,1)}, u32[]{:S(2)}, u32[]{:S(2)}) async-start(bf16[32,3,128,256]{3,2,1,0:T(8,128)(2,1)} %bitcast.31), calls=%async_computation.1 | async-start | bytes 12582912 | tf_op jit(solution)/shard_map/all_to_all | solution.py:211
  238.7 0.0 reduce-scatter.2.cloned.1.call-start
  238.8 0.0 copy-done.4
  238.8 0.1 copy.20
  238.9 0.1 ge.15
  239.0 2.0 sort.32
  241.1 136.2 %all-to-all-done.1 = bf16[32,3,128,256]{3,2,1,0:T(8,128)(2,1)} async-done(((bf16[32,3,128,256]{3,2,1,0:T(8,128)(2,1)}), bf16[32,3,128,256]{3,2,1,0:T(8,128)(2,1)}, u32[]{:S(2)}, u32[]{:S(2)}) %all-to-all-start.1) | async-done | bytes 6291488 | tf_op jit(solution)/shard_map/all_to_all | solution.py:211
  377.3 8.7 %shard_map.132 = bf16[24,128,256]{2,1,0:T(8,128)(2,1)} custom-call(s32[48]{0:T(128)} %get-tuple-element.7.order_ref, s32[48]{0:T(128)} %take_ref.1, s32[48]{0:T(128)} %put_ref.3, s32[1]{0:T(128)} %copy.25.count_ref, bf16[48,128,128]{2,1,0:T(8,128)(2,1)} %adj_ref.3, bf16[96,128,256]{2,1,0:T(8,128)(2,1)} %bitcast.7.operand_ref), custom_call_target="tpu_custom_call" | custom-call | flops 402653184 | bytes 9437184 | tf_op jit(solution)/shard_map/pallas_call | solution.py:64
  386.0 2.3 copy.24
  388.3 3.2 convolution_convert_fusion
  391.5 0.0 reduce-scatter.2.cloned.1.call-update
  391.5 0.1 reshape.113
  391.6 0.0 copy-start.2
  391.6 3.0 gather_fusion.1
  394.6 0.0 copy-done.2
  394.6 0.6 convolution_bitcast_fusion
  395.2 0.3 reshape.114
  395.6 37.0 %all_to_all.20 = f32[256,2,256]{2,1,0:T(2,128)S(1)} all-to-all(f32[256,2,256]{2,1,0:T(2,128)S(1)} %reshape.114), channel_id=1, replica_groups=mesh['row'=8,'col'=32] {'row','col'}, dimensions={0} | all-to-all | bytes 1048576 | tf_op jit(solution)/shard_map/all_to_all | solution.py:144
  432.6 0.3 reduce_sum.19
  432.9 0.1 broadcast_in_dim.30
  433.0 26.6 %all_to_all.21 = f32[256,2,256]{2,1,0:T(2,128)S(1)} all-to-all(f32[256,2,256]{2,1,0:T(2,128)S(1)} %broadcast_in_dim.30), channel_id=1, replica_groups=mesh['row'=8,'col'=32] {'row','col'}, dimensions={0} | all-to-all | bytes 1048576 | tf_op jit(solution)/shard_map/all_to_all | solution.py:148
  459.6 0.1 slice_multiply_fusion
  459.7 0.9 mul.46
  460.6 0.4 reshape.115
  461.0 0.6 slice_multiply_fusion.1
  461.5 0.0 reduce-scatter.2.cloned.1.call-done
  461.5 1.3 convert_element_type.31
  462.8 1.1 convolution_convert_fusion.2
  (9 shorter events, 0.1 us)
Async XLA Ops:
  7.2 41.5 %copy-start = (bf16[256,256]{1,0:T(8,128)(2,1)S(1)}, bf16[256,256]{1,0:T(8,128)(2,1)}, u32[]{:S(2)}) copy-start(bf16[256,256]{1,0:T(8,128)(2,1)} %param.11) | copy-start | bytes 393220
  7.2 41.5 %all-gather.2.cloned.1.call-start = ((), (), s32[]{:S(2)}) async-start(), calls=%async_computation.5 | async-start | bytes 4718592 | tf_op jit(solution)/shard_map/all_gather | solution.py:175
  63.3 12.1 %copy-start.5 = (s32[32,3]{0,1:T(4,128)S(1)}, s32[32,3]{0,1:T(4,128)}, u32[]{:S(2)}) copy-start(s32[32,3]{0,1:T(4,128)} %param.18) | copy-start | bytes 1156
  63.3 154.5 %all-to-all-start = ((bf16[32,3,128,256]{3,2,1,0:T(8,128)(2,1)}), bf16[32,3,128,256]{3,2,1,0:T(8,128)(2,1)}, u32[]{:S(2)}, u32[]{:S(2)}) async-start(bf16[32,3,128,256]{3,2,1,0:T(8,128)(2,1)} %bitcast.33), calls=%async_computation | async-start | bytes 12582912 | tf_op jit(solution)/shard_map/all_to_all | solution.py:196
  222.0 1.0 copy-start.3
  222.0 1.0 copy-start.6
  225.8 2.7 copy-start.1
  228.4 10.4 %copy-start.4 = (s32[8,3]{0,1:T(4,128)S(1)}, s32[8,3]{0,1:T(4,128)}, u32[]{:S(2)}) copy-start(s32[8,3]{0,1:T(4,128)} %param.17) | copy-start | bytes 292
  228.4 148.8 %all-to-all-start.1 = ((bf16[32,3,128,256]{3,2,1,0:T(8,128)(2,1)}), bf16[32,3,128,256]{3,2,1,0:T(8,128)(2,1)}, u32[]{:S(2)}, u32[]{:S(2)}) async-start(bf16[32,3,128,256]{3,2,1,0:T(8,128)(2,1)} %bitcast.31), calls=%async_computation.1 | async-start | bytes 12582912 | tf_op jit(solution)/shard_map/all_to_all | solution.py:211
  238.7 222.8 %reduce-scatter.2.cloned.1.call-start = ((), (), s32[]{:S(2)}) async-start(), calls=%async_computation.6 | async-start | bytes 4718592 | tf_op jit(solution)/shard_map/reduce_scatter | solution.py:234
  391.6 3.0 copy-start.2
Sparse Core Ops, SparseCore 0:
  9.8 38.7 all-gather.1
  391.6 46.2 reduce-scatter.1
